TPU v7x, 32 devices: a whole 2x2x4 slice. The times are simulated.
32 devices in a mesh: groups: 2 (over x), blocks: 16 (over z, y, core).
Axes of the slice: x: 2, y: 2, z: 4, core: 2. Of those that a mesh axis runs over, the one named last changes fastest.
Arguments:
- source_coords: bfloat16 [30, 32768], P(None, ('groups', 'blocks')), parts along dimension 1
- target_coords: bfloat16 [30, 32768], P(None, ('groups', 'blocks')), parts along dimension 1
- target_potential: float32 [32768], P(('groups', 'blocks')), parts along dimension 0, may hold values from -8 to 8
- fetch_blocks: int32 [32, 16, 2], P(('groups', 'blocks')), parts along dimension 0, may hold values from 0 to 127, as said below
- pair_slots: int32 [256, 32], P(('groups', 'blocks')), parts along dimension 0, may hold values from 0 to 31, as said below
- pair_counts: int32 [256], P(('groups', 'blocks')), parts along dimension 0, may hold values from 1 to 32
Outputs:
- source_potential: float32 [32768], P(('groups', 'blocks')), parts along dimension 0
- target_potential_out: float32 [32768], P(('groups', 'blocks')), parts along dimension 0
- drift: float32 [30, 32768], P(None, ('groups', 'blocks')), parts along dimension 1
There are 2 independent parts, one for each index of `groups`. A program takes and returns all parts, laid end to end along the dimension named above; each array names one. Nothing has to cross between parts.
Inputs may be any that keep to these rules, and one draw needn't show every extreme that they name: `fetch_blocks`: entry [d, o, c] is a target block owned by device o, that is between o * 8 and o * 8 + 7; the 2 entries of one [d, o] are distinct. `pair_slots`: entry [s, p] names entry (o, c) of the fetch list of device s // 8 as o * 2 + c; the 32 entries of a row are distinct; entries at p >= pair_counts[s] are unused.
All inputs are finite; a program needn't handle non-finite values.
Results may differ from a plain program's by a relative error of at most 0.00095.
Values may be sent and summed in bfloat16 or wider, within the bound.
No kernel may reach another device: no remote copies, remote signals or barrier semaphores. Data moves between devices by JAX's collectives and lax.ppermute only.
A program may use at most 64 MiB of HBM per device.

v0:
```python
import math

import jax
import jax.numpy as jnp
from jax import lax
from jax.sharding import PartitionSpec as P

SWEEPS = 2


cost_scale = 0.25
floor_value = -1e30


def local(source_coords, target_coords, target_potential, fetch_blocks, pair_slots, pair_counts):
    components = source_coords.shape[0]
    blocks_here = pair_counts.shape[0]
    block_cells = source_coords.shape[1] // blocks_here
    peer_count = lax.axis_size("blocks")
    capacity = fetch_blocks.shape[2]
    slot_count = peer_count * capacity
    most_pairs = pair_slots.shape[1]
    log_mass = -math.log(peer_count * blocks_here * block_cells)
    wanted = fetch_blocks[0]
    asked = lax.all_to_all(wanted, "blocks", split_axis=0, concat_axis=0, tiled=True)
    asked_local = (asked % blocks_here).reshape(-1)
    wanted_flat = wanted.reshape(-1)
    everything = lax.all_gather(target_coords, "blocks", axis=1, tiled=True)
    everything = everything.reshape(components, -1, block_cells)
    slot_coords = jnp.transpose(everything[:, wanted_flat, :], (1, 0, 2))

    def fetch_potentials(potential_here):
        whole_field = lax.all_gather(potential_here, "blocks", axis=0, tiled=True)
        return whole_field[wanted_flat]

    source_layout = source_coords.reshape(components, blocks_here, block_cells)
    source_wide = source_layout.astype(jnp.float32)
    source_norms = jnp.sum(source_wide * source_wide, axis=0)
    slot_wide = slot_coords.astype(jnp.float32)
    slot_norms = jnp.sum(slot_wide * slot_wide, axis=1)
    allowed = jnp.arange(most_pairs, dtype=jnp.int32)[None, :] < pair_counts[:, None]
    per_turn = min(4, most_pairs)
    turn_total = most_pairs // per_turn
    flat_slots = pair_slots.reshape(-1)

    def turn_major(values):
        shaped = values.reshape((blocks_here, turn_total, per_turn) + values.shape[2:])
        return jnp.swapaxes(shaped, 0, 1)

    picked_turns = turn_major(slot_coords[pair_slots])
    norm_turns = turn_major(slot_norms[pair_slots])
    usable_turns = turn_major(allowed)

    def spans_of(picked, norms):
        products = jnp.einsum(
            "dsi,spdj->spij", source_layout, picked, preferred_element_type=jnp.float32
        )
        return (source_norms[:, None, :, None] + norms[:, :, None, :] - 2.0 * products) * cost_scale

    def row_pass(slot_potential):
        potential_turns = turn_major(slot_potential[pair_slots])

        def row_advance(carry, inputs):
            maxima, totals = carry
            picked, norms, usable, potentials = inputs
            mask = usable[:, :, None, None]
            scores = potentials[:, :, None, :] - spans_of(picked, norms)
            tile_max = jnp.max(jnp.where(mask, scores, floor_value), axis=(1, 3))
            raised = jnp.maximum(maxima, tile_max)
            partial_sum = jnp.sum(
                jnp.where(mask, jnp.exp(scores - raised[:, None, :, None]), 0.0), axis=(1, 3)
            )
            return ((raised, totals * jnp.exp(maxima - raised) + partial_sum), None)

        start = (
            jnp.full((blocks_here, block_cells), floor_value, jnp.float32),
            jnp.zeros((blocks_here, block_cells), jnp.float32),
        )
        result, unused = lax.scan(
            row_advance, start, (picked_turns, norm_turns, usable_turns, potential_turns)
        )
        return result

    owned = asked_local[:, None] == jnp.arange(blocks_here, dtype=jnp.int32)[None, :]
    potential_here = target_potential.reshape(blocks_here, block_cells)
    for sweep_index in range(SWEEPS):
        slot_potential = fetch_potentials(potential_here)
        maxima, totals = row_pass(slot_potential)
        source_side = log_mass - (maxima + jnp.log(totals))

        def column_advance(carry, inputs):
            picked, norms, usable = inputs
            mask = usable[:, :, None, None]
            scores = source_side[:, None, :, None] - spans_of(picked, norms)
            pair_max = jnp.max(jnp.where(mask, scores, floor_value), axis=2)
            pair_sum = jnp.sum(
                jnp.where(mask, jnp.exp(scores - pair_max[:, :, None, :]), 0.0), axis=2
            )
            return (carry, (pair_max, pair_sum))

        column_unused, (pair_max, pair_sum) = lax.scan(
            column_advance, 0, (picked_turns, norm_turns, usable_turns)
        )
        pair_max = jnp.swapaxes(pair_max, 0, 1).reshape(-1, block_cells)
        pair_sum = jnp.swapaxes(pair_sum, 0, 1).reshape(-1, block_cells)
        column_maxima = (
            jnp.full((slot_count, block_cells), floor_value, jnp.float32)
            .at[flat_slots]
            .max(pair_max)
        )
        rescaled = pair_sum * jnp.exp(pair_max - column_maxima[flat_slots])
        column_totals = (
            jnp.zeros((slot_count, block_cells), jnp.float32).at[flat_slots].add(rescaled)
        )
        came_max = lax.all_to_all(
            column_maxima.reshape(peer_count, capacity, block_cells),
            "blocks",
            split_axis=0,
            concat_axis=0,
            tiled=True,
        )
        came_total = lax.all_to_all(
            column_totals.reshape(peer_count, capacity, block_cells),
            "blocks",
            split_axis=0,
            concat_axis=0,
            tiled=True,
        )
        came_max = came_max.reshape(slot_count, block_cells)
        came_total = came_total.reshape(slot_count, block_cells)
        merged = jnp.max(jnp.where(owned[:, :, None], came_max[:, None, :], floor_value), axis=0)
        scaled = came_total[:, None, :] * jnp.exp(came_max[:, None, :] - merged[None, :, :])
        summed = jnp.sum(jnp.where(owned[:, :, None], scaled, 0.0), axis=0)
        reached = merged > 0.5 * floor_value
        potential_here = jnp.where(
            reached, log_mass - (merged + jnp.log(jnp.where(reached, summed, 1.0))), potential_here
        )
    slot_potential = fetch_potentials(potential_here)
    maxima, totals = row_pass(slot_potential)
    source_side = log_mass - (maxima + jnp.log(totals))
    row_maxima = maxima
    potential_turns = turn_major(slot_potential[pair_slots])

    def drift_advance(carry, inputs):
        numerator, denominator = carry
        picked, norms, usable, potentials = inputs
        mask = usable[:, :, None, None]
        scores = potentials[:, :, None, :] - spans_of(picked, norms)
        weights = jnp.where(mask, jnp.exp(scores - row_maxima[:, None, :, None]), 0.0).astype(
            jnp.bfloat16
        )
        numerator = numerator + jnp.einsum(
            "spij,spdj->dsi", weights, picked, preferred_element_type=jnp.float32
        )
        denominator = denominator + jnp.sum(weights.astype(jnp.float32), axis=(1, 3))
        return ((numerator, denominator), None)

    start = (
        jnp.zeros((components, blocks_here, block_cells), jnp.float32),
        jnp.zeros((blocks_here, block_cells), jnp.float32),
    )
    (numerator, denominator), unused = lax.scan(
        drift_advance, start, (picked_turns, norm_turns, usable_turns, potential_turns)
    )
    moved = numerator / denominator[None, :, :] - source_wide
    drift = moved.reshape(components, blocks_here * block_cells)
    return (source_side.reshape(-1), potential_here.reshape(-1), drift)


def solution(mesh):
    return jax.shard_map(
        local,
        mesh=mesh,
        in_specs=(
            P(None, ("groups", "blocks")),
            P(None, ("groups", "blocks")),
            P(("groups", "blocks")),
            P(("groups", "blocks"), None, None),
            P(("groups", "blocks"), None),
            P(("groups", "blocks")),
        ),
        out_specs=(P(("groups", "blocks")), P(("groups", "blocks")), P(None, ("groups", "blocks"))),
        check_vma=False,
    )
```

profile of v0, /device:TPU:0, one launch (start us, length us, event | category | flops | bytes accessed | tf_op | source)
XLA Modules:
  0.0 309.9 jit_solution(443387891954823852)
XLA Ops:
  2.0 7.4 %all-to-all-start = ((s32[16,1,2]{2,1,0:T(1,128)}), s32[16,1,2]{2,1,0:T(1,128)S(1)}, u32[]{:S(2)}, u32[]{:S(2)}) async-start(s32[16,1,2]{2,1,0:T(1,128)} %copy.129), calls=%async_computation | async-start | bytes 16384 | tf_op jit(solution)/shard_map/all_to_all | solution.py:25
  11.7 24.9 %all_gather.13 = bf16[30,16384]{1,0:T(8,128)(2,1)S(1)} all-gather(bf16[30,1024]{1,0:T(8,128)(2,1)} %param.19), channel_id=1, replica_groups=mesh['groups'=2,'blocks'=16] {'blocks'}, dimensions={1}, use_global_device_ids=true | all-gather | bytes 1044480 | tf_op jit(solution)/shard_map/all_gather | solution.py:28
  40.1 17.6 %all_gather.12 = f32[128,128]{1,0:T(8,128)S(1)} all-gather(f32[8,128]{1,0:T(8,128)S(1)} %bitcast.329), channel_id=1, replica_groups=mesh['groups'=2,'blocks'=16] {'blocks'}, dimensions={0}, use_global_device_ids=true | all-gather | bytes 69632 | tf_op jit(solution)/shard_map/all_gather | solution.py:33
  59.8 3.6 %copy.135 = bf16[8,8,4,30,128]{4,3,2,1,0:T(8,128)(2,1)} copy(bf16[8,8,4,30,128]{4,2,0,1,3:T(4,128)(2,1)S(1)} %bitcast.301) | data formatting | bytes 3932160
  63.7 29.8 %while.78 = (s32[]{:T(128)}, f32[8,128]{1,0:T(8,128)S(1)}, f32[8,128]{1,0:T(8,128)S(1)}, pred[8,8,4]{1,2,0:T(4,128)(4,1)S(1)}, f32[8,8,4,128]{3,2,1,0:T(4,128)S(...) while((s32[]{:T(128)}, f32[8,128]{1,0:T(8,128)S(1)}, ...), condition=%wide.region_5.6_spmd.clone, body=%wide.region_2.5_spmd.clone.sunk | while | flops 36705280 | bytes 4674368 | solution.py:79
  63.9 3.1 select_reduce_fusion.28
  67.6 3.1 select_reduce_fusion.28
  71.3 3.1 select_reduce_fusion.28
  75.0 3.1 select_reduce_fusion.28
  78.8 3.1 select_reduce_fusion.28
  82.5 3.1 select_reduce_fusion.28
  86.2 3.1 select_reduce_fusion.28
  89.9 3.1 select_reduce_fusion.28
  93.6 18.4 %while.76 = (s32[]{:T(128)}, f32[8,8,4,128]{3,2,1,0:T(4,128)S(1)}, f32[8,8,4,128]{3,2,1,0:T(4,128)S(1)}, pred[8,8,4]{1,2,0:T(4,128)(4,1)S(1)}, f32[8,128]{1,0:T(...) while((s32[]{:T(128)}, f32[8,8,4,128]{3,2,1,0:T(4,128)S(1)}, ...), condition=%wide.region_9.10_spmd, body=%wide.region_6.9_spmd.sunk | while | flops 36691968 | bytes 4690737 | solution.py:101
  98.3 1.7 select_reduce_fusion.24
  100.6 1.7 select_reduce_fusion.24
  102.9 1.7 select_reduce_fusion.24
  109.8 1.7 select_reduce_fusion.24
  112.1 2.0 scatter_custom_fusion
  114.1 3.8 %scatter_custom_fusion.1 = f32[32,128]{1,0:T(8,128)} fusion(s32[256]{0:T(256)S(1)} %bitcast.336, f32[256,128]{1,0:T(8,128)S(1)} %bitcast.313, f32[256,128]{1,0:T(8,128)S(1)} %bitcast.312, f32[]{:T(128)} %constant.151.clone.1, f32[32,128]{1,0:T(8,128)} %scatter_custom_fusion, s32[1024]{0:T(1024)S(1)} %pad_clamp_fusion), kind=kCustom, calls=%fused_computation.119 | custom fusion | flops 98304 | bytes 299012 | tf_op jit(solution)/shard_map/scatter-add | solution.py:113
  117.9 3.5 %all-to-all-start.1 = ((f32[16,2,128]{2,1,0:T(2,128)}), f32[16,2,128]{2,1,0:T(2,128)S(1)}, u32[]{:S(2)}, u32[]{:S(2)}) async-start(f32[16,2,128]{2,1,0:T(2,128)} %bitcast.30), calls=%async_computation.1 | async-start | bytes 32768 | tf_op jit(solution)/shard_map/all_to_all | solution.py:115
  122.8 5.1 %all-to-all-done.1 = f32[16,2,128]{2,1,0:T(2,128)S(1)} async-done(((f32[16,2,128]{2,1,0:T(2,128)}), f32[16,2,128]{2,1,0:T(2,128)S(1)}, u32[]{:S(2)}, u32[]{:S(2)}) %all-to-all-start.1) | async-done | bytes 16416 | tf_op jit(solution)/shard_map/all_to_all | solution.py:115
  127.9 3.5 %all-to-all-start.2 = ((f32[16,2,128]{2,1,0:T(2,128)}), f32[16,2,128]{2,1,0:T(2,128)S(1)}, u32[]{:S(2)}, u32[]{:S(2)}) async-start(f32[16,2,128]{2,1,0:T(2,128)} %bitcast.34), calls=%async_computation.2 | async-start | bytes 32768 | tf_op jit(solution)/shard_map/all_to_all | solution.py:122
  131.5 6.4 %all-to-all-done.2 = f32[16,2,128]{2,1,0:T(2,128)S(1)} async-done(((f32[16,2,128]{2,1,0:T(2,128)}), f32[16,2,128]{2,1,0:T(2,128)S(1)}, u32[]{:S(2)}, u32[]{:S(2)}) %all-to-all-start.2) | async-done | bytes 16416 | tf_op jit(solution)/shard_map/all_to_all | solution.py:122
  138.0 17.9 %all_gather.14 = f32[128,128]{1,0:T(8,128)S(1)} all-gather(f32[8,128]{1,0:T(8,128)S(1)} %subtract_select_fusion.1), channel_id=1, replica_groups=mesh['groups'=2,'blocks'=16] {'blocks'}, dimensions={0}, use_global_device_ids=true | all-gather | bytes 69632 | tf_op jit(solution)/shard_map/all_gather | solution.py:33
  157.2 29.8 %while.79 = (s32[]{:T(128)}, f32[8,128]{1,0:T(8,128)S(1)}, f32[8,128]{1,0:T(8,128)S(1)}, pred[8,8,4]{1,2,0:T(4,128)(4,1)S(1)}, f32[8,8,4,128]{3,2,1,0:T(4,128)S(...) while((s32[]{:T(128)}, f32[8,128]{1,0:T(8,128)S(1)}, ...), condition=%wide.region_17.18_spmd.clone, body=%wide.region_14.17_spmd.clone.sunk | while | flops 36705280 | bytes 4674368 | solution.py:79
  157.3 3.1 select_reduce_fusion.30
  161.1 3.1 select_reduce_fusion.30
  164.8 3.1 select_reduce_fusion.30
  168.5 3.1 select_reduce_fusion.30
  172.2 3.1 select_reduce_fusion.30
  176.0 3.1 select_reduce_fusion.30
  179.7 3.1 select_reduce_fusion.30
  183.4 3.1 select_reduce_fusion.30
  187.1 18.4 %while.77 = (s32[]{:T(128)}, f32[8,8,4,128]{3,2,1,0:T(4,128)S(1)}, f32[8,8,4,128]{3,2,1,0:T(4,128)S(1)}, pred[8,8,4]{1,2,0:T(4,128)(4,1)S(1)}, f32[8,128]{1,0:T(...) while((s32[]{:T(128)}, f32[8,8,4,128]{3,2,1,0:T(4,128)S(1)}, ...), condition=%wide.region_21.22_spmd, body=%wide.region_18.21_spmd.sunk | while | flops 36691968 | bytes 4690737 | solution.py:101
  189.5 1.7 select_reduce_fusion.26
  196.4 1.7 select_reduce_fusion.26
  201.0 1.7 select_reduce_fusion.26
  203.3 1.7 select_reduce_fusion.26
  205.5 2.0 scatter_custom_fusion.2
  207.5 3.5 %all-to-all-start.3 = ((f32[16,2,128]{2,1,0:T(2,128)}), f32[16,2,128]{2,1,0:T(2,128)S(1)}, u32[]{:S(2)}, u32[]{:S(2)}) async-start(f32[16,2,128]{2,1,0:T(2,128)} %bitcast.40), calls=%async_computation.3 | async-start | bytes 32768 | tf_op jit(solution)/shard_map/all_to_all | solution.py:115
  211.0 3.8 %scatter_custom_fusion.3 = f32[32,128]{1,0:T(8,128)} fusion(s32[256]{0:T(256)S(1)} %bitcast.338, f32[256,128]{1,0:T(8,128)S(1)} %bitcast.314, f32[256,128]{1,0:T(8,128)S(1)} %bitcast.310, f32[]{:T(128)} %constant.151.clone.1, f32[32,128]{1,0:T(8,128)} %scatter_custom_fusion.2, s32[1024]{0:T(1024)S(1)} %pad_clamp_fusion), kind=kCustom, calls=%fused_computation.113 | custom fusion | flops 98304 | bytes 299012 | tf_op jit(solution)/shard_map/scatter-add | solution.py:113
  214.9 2.5 all-to-all-done.3
  217.4 3.5 %all-to-all-start.4 = ((f32[16,2,128]{2,1,0:T(2,128)}), f32[16,2,128]{2,1,0:T(2,128)S(1)}, u32[]{:S(2)}, u32[]{:S(2)}) async-start(f32[16,2,128]{2,1,0:T(2,128)} %bitcast.44), calls=%async_computation.4 | async-start | bytes 32768 | tf_op jit(solution)/shard_map/all_to_all | solution.py:122
  221.0 6.4 %all-to-all-done.4 = f32[16,2,128]{2,1,0:T(2,128)S(1)} async-done(((f32[16,2,128]{2,1,0:T(2,128)}), f32[16,2,128]{2,1,0:T(2,128)S(1)}, u32[]{:S(2)}, u32[]{:S(2)}) %all-to-all-start.4) | async-done | bytes 16416 | tf_op jit(solution)/shard_map/all_to_all | solution.py:122
  228.1 17.7 %all_gather.15 = f32[128,128]{1,0:T(8,128)S(1)} all-gather(f32[8,128]{1,0:T(8,128)S(1)} %subtract_select_fusion), channel_id=1, replica_groups=mesh['groups'=2,'blocks'=16] {'blocks'}, dimensions={0}, use_global_device_ids=true | all-gather | bytes 69632 | tf_op jit(solution)/shard_map/all_gather | solution.py:33
  247.2 29.8 %while.80 = (s32[]{:T(128)}, f32[8,128]{1,0:T(8,128)S(1)}, f32[8,128]{1,0:T(8,128)S(1)}, pred[8,8,4]{1,2,0:T(4,128)(4,1)S(1)}, f32[8,8,4,128]{3,2,1,0:T(4,128)S(...) while((s32[]{:T(128)}, f32[8,128]{1,0:T(8,128)S(1)}, ...), condition=%wide.region_29.30_spmd.clone, body=%wide.region_26.29_spmd.clone.sunk | while | flops 36705280 | bytes 4674368 | solution.py:79
  247.3 3.1 select_reduce_fusion.32
  251.0 3.1 select_reduce_fusion.32
  254.8 3.1 select_reduce_fusion.32
  258.5 3.1 select_reduce_fusion.32
  262.2 3.1 select_reduce_fusion.32
  265.9 3.1 select_reduce_fusion.32
  269.7 3.1 select_reduce_fusion.32
  273.4 3.1 select_reduce_fusion.32
  277.0 31.5 %while.81 = (s32[]{:T(128)}, f32[30,8,128]{2,0,1:T(8,128)S(1)}, f32[8,128]{1,0:T(8,128)S(1)}, bf16[8,8,4,30,128]{4,3,2,1,0:T(8,128)(2,1)}, pred[8,8,4]{1,2,0:T(4...) while((s32[]{:T(128)}, f32[30,8,128]{2,0,1:T(8,128)S(1)}, ...), condition=%wide.region_32.33_spmd.clone, body=%wide.region_30.32_spmd.clone.sunk | while | flops 68219904 | bytes 3052840 | solution.py:162
  277.1 2.5 convert_reduce_fusion.2
  281.1 2.5 convert_reduce_fusion.2
  285.0 2.5 convert_reduce_fusion.2
  288.9 2.5 convert_reduce_fusion.2
  292.9 2.5 convert_reduce_fusion.2
  296.8 2.5 convert_reduce_fusion.2
  300.8 2.5 convert_reduce_fusion.2
  304.7 2.5 convert_reduce_fusion.2
  (371 shorter events, 63.8 us)
Async XLA Ops:
  2.0 115.9 %all-to-all-start = ((s32[16,1,2]{2,1,0:T(1,128)}), s32[16,1,2]{2,1,0:T(1,128)S(1)}, u32[]{:S(2)}, u32[]{:S(2)}) async-start(s32[16,1,2]{2,1,0:T(1,128)} %copy.129), calls=%async_computation | async-start | bytes 16384 | tf_op jit(solution)/shard_map/all_to_all | solution.py:25
  38.4 1.7 copy-start.1
  59.8 3.7 %copy-start = (bf16[30,1024]{1,0:T(8,128)(2,1)S(1)}, bf16[30,1024]{1,0:T(8,128)(2,1)}, u32[]{:S(2)}) copy-start(bf16[30,1024]{1,0:T(8,128)(2,1)} %param.18) | copy-start | bytes 184324
  59.8 3.8 %copy-start.2 = (s32[8]{0:T(128)S(1)}, s32[8]{0:T(128)}, u32[]{:S(2)}) copy-start(s32[8]{0:T(128)} %param.23) | copy-start | bytes 100
  117.9 10.0 %all-to-all-start.1 = ((f32[16,2,128]{2,1,0:T(2,128)}), f32[16,2,128]{2,1,0:T(2,128)S(1)}, u32[]{:S(2)}, u32[]{:S(2)}) async-start(f32[16,2,128]{2,1,0:T(2,128)} %bitcast.30), calls=%async_computation.1 | async-start | bytes 32768 | tf_op jit(solution)/shard_map/all_to_all | solution.py:115
  127.9 10.0 %all-to-all-start.2 = ((f32[16,2,128]{2,1,0:T(2,128)}), f32[16,2,128]{2,1,0:T(2,128)S(1)}, u32[]{:S(2)}, u32[]{:S(2)}) async-start(f32[16,2,128]{2,1,0:T(2,128)} %bitcast.34), calls=%async_computation.2 | async-start | bytes 32768 | tf_op jit(solution)/shard_map/all_to_all | solution.py:122
  207.5 10.0 %all-to-all-start.3 = ((f32[16,2,128]{2,1,0:T(2,128)}), f32[16,2,128]{2,1,0:T(2,128)S(1)}, u32[]{:S(2)}, u32[]{:S(2)}) async-start(f32[16,2,128]{2,1,0:T(2,128)} %bitcast.40), calls=%async_computation.3 | async-start | bytes 32768 | tf_op jit(solution)/shard_map/all_to_all | solution.py:115
  217.4 10.0 %all-to-all-start.4 = ((f32[16,2,128]{2,1,0:T(2,128)}), f32[16,2,128]{2,1,0:T(2,128)S(1)}, u32[]{:S(2)}, u32[]{:S(2)}) async-start(f32[16,2,128]{2,1,0:T(2,128)} %bitcast.44), calls=%async_computation.4 | async-start | bytes 32768 | tf_op jit(solution)/shard_map/all_to_all | solution.py:122
where the time goes:
time: 314 us; the launch traced here: 310 us
  matrix products  131 us (42%)
  blocking collectives  78.1 us (25%)
  other arithmetic  33.5 us (11%)
  local copies, waits for them, and re-layouts  21.9 us (7%)
  starting transfers between devices  21.4 us (7%)
  waiting for transfers between devices  20.4 us (6%)
    dot_general x48, matrix products, spans_of(): jnp.einsum('dsi,spdj->spij', source_layout, picked, preferred_element_typ...  121 us
    all_gather x3, blocking collectives, fetch_potentials(): whole_field = lax.all_gather(potential_here, 'blocks', axis=0, tiled=True)  53.2 us
    all_gather x1, blocking collectives, local(): everything = lax.all_gather(target_coords, 'blocks', axis=1, tiled=True)  24.9 us
    all_to_all x2, waiting for transfers between devices, local(): lax.all_to_all(column_totals.reshape(peer_count, capacity, block_cells),...  12.7 us
    reduce_sum x24, other arithmetic, row_advance(): jnp.sum(jnp.where(mask, jnp.exp(scores - raised[:, None, :, None]), 0.0),...  11.2 us
    dot_general x8, matrix products, drift_advance(): jnp.einsum('spij,spdj->dsi', weights, picked, preferred_element_type=jnp....  9.83 us
    scatter-add x2, other arithmetic, local(): jnp.zeros((slot_count, block_cells), jnp.float32).at[flat_slots]  7.69 us
    all_to_all x2, waiting for transfers between devices, local(): lax.all_to_all(column_maxima.reshape(peer_count, capacity, block_cells),...  7.65 us
  transfers between devices with their start and end apart: 5, of which 4 were waited for; matrix products, arithmetic and copies ran while one was open for 23% of the time, Pallas kernels for 0%

commit v1 on v0

v1 whole, which is shorter than its diff:
```python
import functools
import math

import jax
import jax.numpy as jnp
from jax import lax
from jax.experimental import pallas as pl
from jax.experimental.pallas import tpu as pltpu
from jax.sharding import PartitionSpec as P

SWEEPS = 2

floor_value = -1e30
PADDED = 32


def _slot_offsets(y_ref, g_ref, h_ref, ncomp):
    rows = lax.broadcasted_iota(jnp.int32, y_ref.shape[1:], 0)

    def one(t, c):
        yf = y_ref[t].astype(jnp.float32)
        sq = jnp.where(rows < ncomp, yf * yf, 0.0)
        ny = jnp.sum(sq, axis=0, keepdims=True)
        h_ref[t] = g_ref[t] - 0.25 * ny
        return c

    lax.fori_loop(0, y_ref.shape[0], one, 0)


def _row_scores(s, cnt, slots_ref, xs, y_ref, h_ref, s_ref, most, bs):
    def first(p, m):
        sl = slots_ref[s * most + p]
        prod = jnp.dot(xs, y_ref[sl], preferred_element_type=jnp.float32)
        sc = prod + h_ref[sl]
        s_ref[p] = sc
        return jnp.maximum(m, sc)

    m = lax.fori_loop(0, cnt, first, jnp.full((bs, bs), floor_value, jnp.float32))
    return jnp.max(m, axis=1, keepdims=True)


def sweep_kernel(slots_ref, counts_ref, xT_ref, y_ref, g_ref, amax_ref, asum_ref, h_ref, s_ref, *, most, log_mass, ncomp):
    nblk, bs = xT_ref.shape[0], xT_ref.shape[1]
    _slot_offsets(y_ref, g_ref, h_ref, ncomp)
    amax_ref[...] = jnp.full(amax_ref.shape, floor_value, jnp.float32)
    asum_ref[...] = jnp.zeros(asum_ref.shape, jnp.float32)

    def block(s, carry):
        cnt = counts_ref[s]
        xs = xT_ref[s]
        mrow = _row_scores(s, cnt, slots_ref, xs, y_ref, h_ref, s_ref, most, bs)
        mb = jnp.broadcast_to(mrow, (bs, bs))

        def second(p, acc):
            return acc + jnp.exp(s_ref[p] - mb)

        acc = lax.fori_loop(0, cnt, second, jnp.zeros((bs, bs), jnp.float32))
        tot = jnp.sum(acc, axis=1, keepdims=True)
        kb = jnp.broadcast_to(log_mass - (mrow + jnp.log(tot)), (bs, bs))

        def column(p, c):
            sl = slots_ref[s * most + p]
            v = s_ref[p] + kb
            cm = jnp.max(v, axis=0, keepdims=True)
            ce = jnp.sum(jnp.exp(v - cm), axis=0, keepdims=True)
            tm = cm - g_ref[sl]
            om = amax_ref[sl]
            nm = jnp.maximum(om, tm)
            asum_ref[sl] = asum_ref[sl] * jnp.exp(om - nm) + ce * jnp.exp(tm - nm)
            amax_ref[sl] = nm
            return c

        lax.fori_loop(0, cnt, column, 0)
        return carry

    lax.fori_loop(0, nblk, block, 0)


def final_kernel(slots_ref, counts_ref, xT_ref, x_ref, y_ref, g_ref, f_ref, drift_ref, h_ref, s_ref, *, most, log_mass, ncomp):
    nblk, bs = xT_ref.shape[0], xT_ref.shape[1]
    _slot_offsets(y_ref, g_ref, h_ref, ncomp)

    def block(s, carry):
        cnt = counts_ref[s]
        xs = xT_ref[s]
        mrow = _row_scores(s, cnt, slots_ref, xs, y_ref, h_ref, s_ref, most, bs)
        mb = jnp.broadcast_to(mrow, (bs, bs))

        def second(p, c):
            acc, num = c
            sl = slots_ref[s * most + p]
            e = jnp.exp(s_ref[p] - mb)
            w = e.astype(jnp.bfloat16)
            num = num + lax.dot_general(
                y_ref[sl], w, (((1,), (1,)), ((), ())), preferred_element_type=jnp.float32
            )
            return acc + e, num

        acc, num = lax.fori_loop(
            0,
            cnt,
            second,
            (jnp.zeros((bs, bs), jnp.float32), jnp.zeros((y_ref.shape[1], bs), jnp.float32)),
        )
        tot = jnp.sum(acc, axis=1, keepdims=True)
        xf = xs.astype(jnp.float32)
        quarter_nx = jnp.sum(xf * xf, axis=1, keepdims=True)
        fcol = log_mass - (mrow + jnp.log(tot)) + quarter_nx
        frow = jnp.transpose(jnp.broadcast_to(fcol, (bs, bs)))[0:1, :]
        f_ref[s] = frow
        off = pl.multiple_of(s * bs, bs)
        xcols = x_ref[:, pl.ds(off, bs)].astype(jnp.float32)
        drift_ref[:, pl.ds(off, bs)] = num[:ncomp] / num[ncomp : ncomp + 1] - xcols
        return carry

    lax.fori_loop(0, nblk, block, 0)


def _specs(kinds):
    return [pl.BlockSpec(memory_space=pltpu.SMEM if k == "s" else pltpu.VMEM) for k in kinds]


def local(source_coords, target_coords, target_potential, fetch_blocks, pair_slots, pair_counts):
    ncomp = source_coords.shape[0]
    nblk = pair_counts.shape[0]
    bs = source_coords.shape[1] // nblk
    peers = lax.axis_size("blocks")
    cap = fetch_blocks.shape[2]
    nslot = peers * cap
    most = pair_slots.shape[1]
    log_mass = -math.log(peers * nblk * bs)

    wanted = fetch_blocks[0]
    asked = lax.all_to_all(wanted, "blocks", split_axis=0, concat_axis=0, tiled=True)
    asked_local = (asked % nblk).reshape(-1)

    target_blocks = jnp.transpose(target_coords.reshape(ncomp, nblk, bs), (1, 0, 2))
    send_coords = target_blocks[asked_local].reshape(peers, cap, ncomp, bs)
    potential_here = target_potential.reshape(nblk, bs)
    send_potential = potential_here[asked_local].reshape(peers, cap, bs)
    came_coords = lax.all_to_all(send_coords, "blocks", split_axis=0, concat_axis=0, tiled=True)
    slot_potential = lax.all_to_all(send_potential, "blocks", split_axis=0, concat_axis=0, tiled=True)
    slot_potential = slot_potential.reshape(nslot, 1, bs)
    came_coords = came_coords.reshape(nslot, ncomp, bs)
    slot_coords = jnp.concatenate(
        [
            came_coords,
            jnp.ones((nslot, 1, bs), jnp.bfloat16),
            jnp.zeros((nslot, PADDED - ncomp - 1, bs), jnp.bfloat16),
        ],
        axis=1,
    )
    halved = (source_coords.astype(jnp.float32) * 0.5).astype(jnp.bfloat16)
    halved = jnp.concatenate([halved, jnp.zeros((PADDED - ncomp, nblk * bs), jnp.bfloat16)], axis=0)
    source_rows = jnp.transpose(halved.reshape(PADDED, nblk, bs), (1, 2, 0))
    flat_slots = pair_slots.reshape(-1)

    vmem = 48 * 1024 * 1024
    sweep = pl.pallas_call(
        functools.partial(sweep_kernel, most=most, log_mass=log_mass, ncomp=ncomp),
        out_shape=(jax.ShapeDtypeStruct((nslot, 1, bs), jnp.float32),) * 2,
        in_specs=_specs("ssvvv"),
        out_specs=tuple(_specs("vv")),
        scratch_shapes=[pltpu.VMEM((nslot, 1, bs), jnp.float32), pltpu.VMEM((most, bs, bs), jnp.float32)],
        compiler_params=pltpu.CompilerParams(vmem_limit_bytes=vmem),
    )
    final = pl.pallas_call(
        functools.partial(final_kernel, most=most, log_mass=log_mass, ncomp=ncomp),
        out_shape=(
            jax.ShapeDtypeStruct((nblk, 1, bs), jnp.float32),
            jax.ShapeDtypeStruct((ncomp, nblk * bs), jnp.float32),
        ),
        in_specs=_specs("ssvvvv"),
        out_specs=tuple(_specs("vv")),
        scratch_shapes=[pltpu.VMEM((nslot, 1, bs), jnp.float32), pltpu.VMEM((most, bs, bs), jnp.float32)],
        compiler_params=pltpu.CompilerParams(vmem_limit_bytes=vmem),
    )

    owned = asked_local[:, None] == jnp.arange(nblk, dtype=jnp.int32)[None, :]
    for sweep_index in range(SWEEPS):
        part_max, part_sum = sweep(flat_slots, pair_counts, source_rows, slot_coords, slot_potential)
        parts = jnp.stack([part_max.reshape(nslot, bs), part_sum.reshape(nslot, bs)], axis=1)
        came = lax.all_to_all(
            parts.reshape(peers, cap, 2, bs), "blocks", split_axis=0, concat_axis=0, tiled=True
        ).reshape(nslot, 2, bs)
        came_max = came[:, 0]
        came_sum = came[:, 1]
        merged = jnp.max(jnp.where(owned[:, :, None], came_max[:, None, :], floor_value), axis=0)
        scaled = came_sum[:, None, :] * jnp.exp(came_max[:, None, :] - merged[None, :, :])
        summed = jnp.sum(jnp.where(owned[:, :, None], scaled, 0.0), axis=0)
        reached = merged > 0.5 * floor_value
        potential_here = jnp.where(
            reached, log_mass - (merged + jnp.log(jnp.where(reached, summed, 1.0))), potential_here
        )
        send_potential = potential_here[asked_local].reshape(peers, cap, bs)
        slot_potential = lax.all_to_all(
            send_potential, "blocks", split_axis=0, concat_axis=0, tiled=True
        ).reshape(nslot, 1, bs)

    source_side, drift = final(flat_slots, pair_counts, source_rows, source_coords, slot_coords, slot_potential)
    return (source_side.reshape(-1), potential_here.reshape(-1), drift)


def solution(mesh):
    return jax.shard_map(
        local,
        mesh=mesh,
        in_specs=(
            P(None, ("groups", "blocks")),
            P(None, ("groups", "blocks")),
            P(("groups", "blocks")),
            P(("groups", "blocks"), None, None),
            P(("groups", "blocks"), None),
            P(("groups", "blocks")),
        ),
        out_specs=(P(("groups", "blocks")), P(("groups", "blocks")), P(None, ("groups", "blocks"))),
        check_vma=False,
    )
```

time: 314 us -> 213 us (0.68)
  the two profiles are of different devices: /device:TPU:0 before, /device:TPU:11 now
where the time goes in v1:
time: 213 us; the launch traced here: 210 us
  Pallas kernels  132 us (62%)
  starting transfers between devices  25.1 us (12%)
  waiting for transfers between devices  23.8 us (11%)
  blocking collectives  17.1 us (8%)
  local copies, waits for them, and re-layouts  9.05 us (4%)
  other arithmetic  2.64 us (1%)
    pallas_call x2, Pallas kernels, local(): sweep(flat_slots, pair_counts, source_rows, slot_coords, slot_potential)  75.7 us
    pallas_call x1, Pallas kernels, local(): final(flat_slots, pair_counts, source_rows, source_coords, slot_coords, s...  55.9 us
    all_to_all x2, starting transfers between devices, local(): lax.all_to_all(send_potential, 'blocks', split_axis=0, concat_axis=0, til...  9.83 us
    all_to_all x2, waiting for transfers between devices, local(): lax.all_to_all(send_potential, 'blocks', split_axis=0, concat_axis=0, til...  9.37 us
    all_to_all x1, blocking collectives, local(): lax.all_to_all(send_potential, 'blocks', split_axis=0, concat_axis=0, til...  9.18 us
    all_to_all x1, blocking collectives, local(): lax.all_to_all(parts.reshape(peers, cap, 2, bs), 'blocks', split_axis=0,...  7.88 us
    all_to_all x1, starting transfers between devices, local(): lax.all_to_all(wanted, 'blocks', split_axis=0, concat_axis=0, tiled=True)  6.58 us
    all_to_all x1, waiting for transfers between devices, local(): lax.all_to_all(send_coords, 'blocks', split_axis=0, concat_axis=0, tiled=...  6.06 us
  transfers between devices with their start and end apart: 5, of which 5 were waited for; matrix products, arithmetic and copies ran while one was open for 2% of the time, Pallas kernels for 0%

profile of v1, /device:TPU:11, one launch (start us, length us, event | category | flops | bytes accessed | tf_op | source)
XLA Modules:
  0.0 210.0 jit_solution(13812928623710450445)
XLA Ops:
  0.6 0.0 copy-start.4
  0.6 0.7 copy-done.4
  1.3 0.7 copy.27
  2.0 6.6 %all-to-all-start = ((s32[16,1,2]{2,1,0:T(1,128)}), s32[16,1,2]{2,1,0:T(1,128)S(1)}, u32[]{:S(2)}, u32[]{:S(2)}) async-start(s32[16,1,2]{2,1,0:T(1,128)} %copy.27), calls=%async_computation | async-start | bytes 16384 | tf_op jit(solution)/shard_map/all_to_all | solution.py:134
  8.6 0.8 copy.39
  9.5 3.8 %all-to-all-done = s32[16,1,2]{2,1,0:T(1,128)S(1)} async-done(((s32[16,1,2]{2,1,0:T(1,128)}), s32[16,1,2]{2,1,0:T(1,128)S(1)}, u32[]{:S(2)}, u32[]{:S(2)}) %all-to-all-start) | async-done | bytes 160 | tf_op jit(solution)/shard_map/all_to_all | solution.py:134
  13.2 0.5 broadcast.142
  13.8 0.7 reduce.5
  14.4 0.1 all_to_all.30
  14.6 0.6 gather_fusion
  15.2 0.9 copy.28
  16.0 0.0 copy-start.3
  16.0 0.0 copy-start
  16.0 5.3 %all-to-all-start.1 = ((bf16[16,2,30,128]{3,1,2,0:T(2,128)(2,1)}), bf16[16,2,30,128]{3,1,2,0:T(2,128)(2,1)S(1)}, u32[]{:S(2)}, u32[]{:S(2)}) async-start(bf16[16,2,30,128]{3,1,2,0:T(2,128)(2,1)} %copy.28), calls=%async_computation.1 | async-start | bytes 491520 | tf_op jit(solution)/shard_map/all_to_all | solution.py:141
  21.3 0.0 copy-done.3
  21.3 0.1 reshape.157.slots_ref
  21.4 0.0 copy-done
  21.4 0.2 copy.38
  21.6 0.1 concatenate.6.clone
  21.7 0.0 copy-start.2
  21.7 0.1 pad.7.clone
  21.7 0.1 pad.6.clone
  21.8 0.5 copy-done.2
  22.3 1.2 gather_fusion.1
  23.5 0.1 all_to_all.32
  23.6 6.1 %all-to-all-done.1 = bf16[16,2,30,128]{3,1,2,0:T(2,128)(2,1)S(1)} async-done(((bf16[16,2,30,128]{3,1,2,0:T(2,128)(2,1)}), bf16[16,2,30,128]{3,1,2,0:T(2,128)(2,1)S(1)}, u32[]{:S(2)}, u32[]{:S(2)}) %all-to-all-start.1) | async-done | bytes 245792 | tf_op jit(solution)/shard_map/all_to_all | solution.py:141
  29.7 4.8 %all-to-all-start.2 = ((f32[16,2,128]{2,1,0:T(2,128)}), f32[16,2,128]{2,1,0:T(2,128)S(1)}, u32[]{:S(2)}, u32[]{:S(2)}) async-start(f32[16,2,128]{2,1,0:T(2,128)} %bitcast.9), calls=%async_computation.2 | async-start | bytes 32768 | tf_op jit(solution)/shard_map/all_to_all | solution.py:142
  34.6 0.1 maximum_maximum_fusion.y_ref
  34.7 4.9 %all-to-all-done.2 = f32[16,2,128]{2,1,0:T(2,128)S(1)} async-done(((f32[16,2,128]{2,1,0:T(2,128)}), f32[16,2,128]{2,1,0:T(2,128)S(1)}, u32[]{:S(2)}, u32[]{:S(2)}) %all-to-all-start.2) | async-done | bytes 16416 | tf_op jit(solution)/shard_map/all_to_all | solution.py:142
  39.6 0.0 copy-start.1
  39.6 0.7 copy-done.1
  40.3 37.9 %shard_map.85 = (f32[32,1,128]{2,1,0:T(1,128)S(1)}, f32[32,1,128]{2,1,0:T(1,128)S(1)}) custom-call(s32[256]{0:T(256)S(1)} %reshape.157.slots_ref, s32[8]{0:T(128)S(1)} %copy-done.1, bf16[8,128,32]{2,1,0:T(8,128)(2,1)S(1)} %bitcast.68, bf16[32,32,128]{2,1,0:T(8,128)(2,1)S(1)} %maximum_maximum_fusion.y_ref, f32[32,1,128]{2,1,0:T(1,128)S(1)} %bitcast.72), custom_call_target="tpu_custom_call" | custom-call | tf_op jit(solution)/shard_map/pallas_call | solution.py:181
  78.1 0.6 pad_maximum_fusion
  78.8 3.4 %all-to-all-start.3 = ((f32[16,2,2,128]{3,2,1,0:T(2,128)}), f32[16,2,2,128]{3,2,1,0:T(2,128)S(1)}, u32[]{:S(2)}, u32[]{:S(2)}) async-start(f32[16,2,2,128]{3,2,1,0:T(2,128)} %bitcast.11), calls=%async_computation.3 | async-start | bytes 65536 | tf_op jit(solution)/shard_map/all_to_all | solution.py:183
  82.2 0.1 iota_compare_fusion
  82.2 4.6 %all-to-all-done.3 = f32[16,2,2,128]{3,2,1,0:T(2,128)S(1)} async-done(((f32[16,2,2,128]{3,2,1,0:T(2,128)}), f32[16,2,2,128]{3,2,1,0:T(2,128)S(1)}, u32[]{:S(2)}, u32[]{:S(2)}) %all-to-all-start.3) | async-done | bytes 32800 | tf_op jit(solution)/shard_map/all_to_all | solution.py:183
  86.9 0.1 select_reduce_fusion.3
  87.0 0.1 select_reduce_fusion.2
  87.1 0.6 gather_fusion.2
  87.7 9.2 %all_to_all.45 = f32[16,2,128]{2,1,0:T(2,128)S(1)} all-to-all(f32[16,2,128]{2,1,0:T(2,128)S(1)} %bitcast.83), channel_id=1, replica_groups=mesh['groups'=2,'blocks'=16] {'blocks'}, dimensions={0} | all-to-all | bytes 32768 | tf_op jit(solution)/shard_map/all_to_all | solution.py:196
  96.9 37.9 %shard_map.86 = (f32[32,1,128]{2,1,0:T(1,128)S(1)}, f32[32,1,128]{2,1,0:T(1,128)S(1)}) custom-call(s32[256]{0:T(256)S(1)} %reshape.157.slots_ref, s32[8]{0:T(128)S(1)} %copy-done.1, bf16[8,128,32]{2,1,0:T(8,128)(2,1)S(1)} %bitcast.69, bf16[32,32,128]{2,1,0:T(8,128)(2,1)S(1)} %maximum_maximum_fusion.y_ref, f32[32,1,128]{2,1,0:T(1,128)S(1)} %bitcast.73), custom_call_target="tpu_custom_call" | custom-call | tf_op jit(solution)/shard_map/pallas_call | solution.py:181
  134.8 7.9 %all_to_all.46 = f32[16,2,2,128]{3,2,1,0:T(2,128)S(1)} all-to-all(f32[16,2,2,128]{3,2,1,0:T(2,128)S(1)} %bitcast.81), channel_id=1, replica_groups=mesh['groups'=2,'blocks'=16] {'blocks'}, dimensions={0} | all-to-all | bytes 65536 | tf_op jit(solution)/shard_map/all_to_all | solution.py:183
  142.7 0.1 select_reduce_fusion.1
  142.8 0.1 select_reduce_fusion
  142.9 1.2 gather_fusion.3
  144.1 5.0 %all-to-all-start.6 = ((f32[16,2,128]{2,1,0:T(2,128)}), f32[16,2,128]{2,1,0:T(2,128)S(1)}, u32[]{:S(2)}, u32[]{:S(2)}) async-start(f32[16,2,128]{2,1,0:T(2,128)} %bitcast.21), calls=%async_computation.6 | async-start | bytes 32768 | tf_op jit(solution)/shard_map/all_to_all | solution.py:196
  149.1 0.6 fusion.4
  149.7 4.5 %all-to-all-done.6 = f32[16,2,128]{2,1,0:T(2,128)S(1)} async-done(((f32[16,2,128]{2,1,0:T(2,128)}), f32[16,2,128]{2,1,0:T(2,128)S(1)}, u32[]{:S(2)}, u32[]{:S(2)}) %all-to-all-start.6) | async-done | bytes 16416 | tf_op jit(solution)/shard_map/all_to_all | solution.py:196
  154.2 55.9 %shard_map.87 = (f32[8,1,128]{2,1,0:T(1,128)}, f32[30,1024]{1,0:T(8,128)}) custom-call(s32[256]{0:T(256)S(1)} %reshape.157.slots_ref, s32[8]{0:T(128)S(1)} %copy-done.1, bf16[8,128,32]{2,1,0:T(8,128)(2,1)S(1)} %bitcast.70, bf16[30,1024]{1,0:T(8,128)(2,1)S(1)} %copy-done, bf16[32,32,128]{2,1,0:T(8,128)(2,1)S(1)} %maximum_maximum_fusion.y_ref, ...), custom_call_target="tpu_custom_call" | custom-call | tf_op jit(solution)/shard_map/pallas_call | solution.py:200
  (12 shorter events, 0.2 us)
Async XLA Ops:
  0.6 0.7 copy-start.4
  2.0 11.3 %all-to-all-start = ((s32[16,1,2]{2,1,0:T(1,128)}), s32[16,1,2]{2,1,0:T(1,128)S(1)}, u32[]{:S(2)}, u32[]{:S(2)}) async-start(s32[16,1,2]{2,1,0:T(1,128)} %copy.27), calls=%async_computation | async-start | bytes 16384 | tf_op jit(solution)/shard_map/all_to_all | solution.py:134
  16.0 5.3 %copy-start.3 = (s32[8,32]{1,0:T(8,128)S(1)}, s32[8,32]{1,0:T(8,128)}, u32[]{:S(2)}) copy-start(s32[8,32]{1,0:T(8,128)} %param.10) | copy-start | bytes 3076
  16.0 5.3 %copy-start = (bf16[30,1024]{1,0:T(8,128)(2,1)S(1)}, bf16[30,1024]{1,0:T(8,128)(2,1)}, u32[]{:S(2)}) copy-start(bf16[30,1024]{1,0:T(8,128)(2,1)} %x_ref.1) | copy-start | bytes 184324
  16.0 13.6 %all-to-all-start.1 = ((bf16[16,2,30,128]{3,1,2,0:T(2,128)(2,1)}), bf16[16,2,30,128]{3,1,2,0:T(2,128)(2,1)S(1)}, u32[]{:S(2)}, u32[]{:S(2)}) async-start(bf16[16,2,30,128]{3,1,2,0:T(2,128)(2,1)} %copy.28), calls=%async_computation.1 | async-start | bytes 491520 | tf_op jit(solution)/shard_map/all_to_all | solution.py:141
  21.7 0.7 copy-start.2
  29.7 9.9 %all-to-all-start.2 = ((f32[16,2,128]{2,1,0:T(2,128)}), f32[16,2,128]{2,1,0:T(2,128)S(1)}, u32[]{:S(2)}, u32[]{:S(2)}) async-start(f32[16,2,128]{2,1,0:T(2,128)} %bitcast.9), calls=%async_computation.2 | async-start | bytes 32768 | tf_op jit(solution)/shard_map/all_to_all | solution.py:142
  39.6 0.7 copy-start.1
  78.8 8.1 %all-to-all-start.3 = ((f32[16,2,2,128]{3,2,1,0:T(2,128)}), f32[16,2,2,128]{3,2,1,0:T(2,128)S(1)}, u32[]{:S(2)}, u32[]{:S(2)}) async-start(f32[16,2,2,128]{3,2,1,0:T(2,128)} %bitcast.11), calls=%async_computation.3 | async-start | bytes 65536 | tf_op jit(solution)/shard_map/all_to_all | solution.py:183
  144.1 10.1 %all-to-all-start.6 = ((f32[16,2,128]{2,1,0:T(2,128)}), f32[16,2,128]{2,1,0:T(2,128)S(1)}, u32[]{:S(2)}, u32[]{:S(2)}) async-start(f32[16,2,128]{2,1,0:T(2,128)} %bitcast.21), calls=%async_computation.6 | async-start | bytes 32768 | tf_op jit(solution)/shard_map/all_to_all | solution.py:196

commit v2 on v1

v2 whole, which is shorter than its diff:
```python
import functools
import math

import jax
import jax.numpy as jnp
from jax import lax
from jax.experimental import pallas as pl
from jax.experimental.pallas import tpu as pltpu
from jax.sharding import PartitionSpec as P

SWEEPS = 2

floor_value = -1e30
PADDED = 32
CHUNK = 4


def _slot_offsets(y_ref, g_ref, h_ref, ncomp):
    rows = lax.broadcasted_iota(jnp.int32, y_ref.shape[1:], 0)

    def one(t, c):
        yf = y_ref[t].astype(jnp.float32)
        sq = jnp.where(rows < ncomp, yf * yf, 0.0)
        ny = jnp.sum(sq, axis=0, keepdims=True)
        h_ref[t] = g_ref[t] - 0.25 * ny
        return c

    lax.fori_loop(0, y_ref.shape[0], one, 0)


def _chunk_slots(slots_ref, s, q, most):
    return [slots_ref[s * most + jnp.minimum(q * CHUNK + c, most - 1)] for c in range(CHUNK)]


def _lane_fold(v, bs, op):
    out = v[:, 0:bs]
    for c in range(1, CHUNK):
        out = op(out, v[:, c * bs : (c + 1) * bs])
    return out


def _row_scores(s, cnt, slots_ref, xs, y_ref, h_ref, s_ref, most, bs):
    lane_tile = lax.broadcasted_iota(jnp.int32, (1, CHUNK * bs), 1) // bs

    def first(q, m):
        sls = _chunk_slots(slots_ref, s, q, most)
        rhs = jnp.concatenate([y_ref[sl] for sl in sls], axis=1)
        hrow = jnp.concatenate([h_ref[sl] for sl in sls], axis=1)
        prod = jnp.dot(xs, rhs, preferred_element_type=jnp.float32)
        sc = jnp.where(lane_tile + q * CHUNK < cnt, prod + hrow, floor_value)
        s_ref[q] = sc
        return jnp.maximum(m, _lane_fold(sc, bs, jnp.maximum))

    nq = (cnt + CHUNK - 1) // CHUNK
    m = lax.fori_loop(0, nq, first, jnp.full((bs, bs), floor_value, jnp.float32))
    return nq, jnp.max(m, axis=1, keepdims=True)


def sweep_kernel(slots_ref, counts_ref, xT_ref, y_ref, g_ref, amax_ref, asum_ref, h_ref, s_ref, *, most, log_mass, ncomp):
    nblk, bs = xT_ref.shape[0], xT_ref.shape[1]
    _slot_offsets(y_ref, g_ref, h_ref, ncomp)
    amax_ref[...] = jnp.full(amax_ref.shape, floor_value, jnp.float32)
    asum_ref[...] = jnp.zeros(asum_ref.shape, jnp.float32)

    def block(s, carry):
        cnt = counts_ref[s]
        nq, mrow = _row_scores(s, cnt, slots_ref, xT_ref[s], y_ref, h_ref, s_ref, most, bs)
        mb = jnp.concatenate([jnp.broadcast_to(mrow, (bs, bs))] * CHUNK, axis=1)

        def second(q, acc):
            return acc + _lane_fold(jnp.exp(s_ref[q] - mb), bs, jnp.add)

        acc = lax.fori_loop(0, nq, second, jnp.zeros((bs, bs), jnp.float32))
        tot = jnp.sum(acc, axis=1, keepdims=True)
        kb = jnp.concatenate([jnp.broadcast_to(log_mass - (mrow + jnp.log(tot)), (bs, bs))] * CHUNK, axis=1)

        def column(q, c):
            sls = _chunk_slots(slots_ref, s, q, most)
            v = s_ref[q] + kb
            cm = jnp.max(v, axis=0, keepdims=True)
            ce = jnp.sum(jnp.exp(v - cm), axis=0, keepdims=True)
            for t, sl in enumerate(sls):
                @pl.when(q * CHUNK + t < cnt)
                def _():
                    tm = cm[:, t * bs : (t + 1) * bs] - g_ref[sl]
                    om = amax_ref[sl]
                    nm = jnp.maximum(om, tm)
                    asum_ref[sl] = asum_ref[sl] * jnp.exp(om - nm) + ce[:, t * bs : (t + 1) * bs] * jnp.exp(tm - nm)
                    amax_ref[sl] = nm
            return c

        lax.fori_loop(0, nq, column, 0)
        return carry

    lax.fori_loop(0, nblk, block, 0)


def final_kernel(slots_ref, counts_ref, xT_ref, x_ref, y_ref, yT_ref, g_ref, f_ref, drift_ref, h_ref, s_ref, *, most, log_mass, ncomp):
    nblk, bs = xT_ref.shape[0], xT_ref.shape[1]
    _slot_offsets(y_ref, g_ref, h_ref, ncomp)
    lanes = lax.broadcasted_iota(jnp.int32, (bs, yT_ref.shape[2]), 1)

    def block(s, carry):
        cnt = counts_ref[s]
        xs = xT_ref[s]
        nq, mrow = _row_scores(s, cnt, slots_ref, xs, y_ref, h_ref, s_ref, most, bs)
        mb = jnp.concatenate([jnp.broadcast_to(mrow, (bs, bs))] * CHUNK, axis=1)

        def second(q, c):
            acc, num = c
            sls = _chunk_slots(slots_ref, s, q, most)
            e = jnp.exp(s_ref[q] - mb)
            w = e.astype(jnp.bfloat16)
            rhs = jnp.concatenate([yT_ref[sl] for sl in sls], axis=0)
            num = num + jnp.dot(w, rhs, preferred_element_type=jnp.float32)
            return acc + _lane_fold(e, bs, jnp.add), num

        acc, num = lax.fori_loop(
            0,
            nq,
            second,
            (jnp.zeros((bs, bs), jnp.float32), jnp.zeros((bs, yT_ref.shape[2]), jnp.float32)),
        )
        tot = jnp.sum(acc, axis=1, keepdims=True)
        xf = xs.astype(jnp.float32)
        quarter_nx = jnp.sum(xf * xf, axis=1, keepdims=True)
        fcol = log_mass - (mrow + jnp.log(tot)) + quarter_nx
        packed = jnp.where(lanes == PADDED - 1, jnp.broadcast_to(fcol, num.shape), num)
        rows = jnp.transpose(packed)
        f_ref[s] = rows[PADDED - 1 : PADDED, :]
        off = pl.multiple_of(s * bs, bs)
        xcols = x_ref[:, pl.ds(off, bs)].astype(jnp.float32)
        drift_ref[:, pl.ds(off, bs)] = rows[:ncomp] / rows[ncomp : ncomp + 1] - xcols
        return carry

    lax.fori_loop(0, nblk, block, 0)


def _specs(kinds):
    return [pl.BlockSpec(memory_space=pltpu.SMEM if k == "s" else pltpu.VMEM) for k in kinds]


def local(source_coords, target_coords, target_potential, fetch_blocks, pair_slots, pair_counts):
    ncomp = source_coords.shape[0]
    nblk = pair_counts.shape[0]
    bs = source_coords.shape[1] // nblk
    peers = lax.axis_size("blocks")
    cap = fetch_blocks.shape[2]
    nslot = peers * cap
    most = pair_slots.shape[1]
    log_mass = -math.log(peers * nblk * bs)
    chunks = (most + CHUNK - 1) // CHUNK

    wanted = fetch_blocks[0]
    asked = lax.all_to_all(wanted, "blocks", split_axis=0, concat_axis=0, tiled=True)
    asked_local = (asked % nblk).reshape(-1)

    potential_here = target_potential.reshape(nblk, bs)
    target_blocks = jnp.concatenate(
        [jnp.transpose(target_coords.reshape(ncomp, nblk, bs).astype(jnp.float32), (1, 0, 2)), potential_here[:, None, :]],
        axis=1,
    )
    send = target_blocks[asked_local].reshape(peers, cap, ncomp + 1, bs)
    came = lax.all_to_all(send, "blocks", split_axis=0, concat_axis=0, tiled=True).reshape(nslot, ncomp + 1, bs)
    slot_potential = came[:, ncomp:, :]
    came_coords = came[:, :ncomp, :].astype(jnp.bfloat16)
    slot_coords = jnp.concatenate(
        [
            came_coords,
            jnp.ones((nslot, 1, bs), jnp.bfloat16),
            jnp.zeros((nslot, PADDED - ncomp - 1, bs), jnp.bfloat16),
        ],
        axis=1,
    )
    slot_rows = jnp.concatenate(
        [jnp.transpose(slot_coords, (0, 2, 1)), jnp.zeros((nslot, bs, bs - PADDED), jnp.bfloat16)], axis=2
    )
    halved = (source_coords.astype(jnp.float32) * 0.5).astype(jnp.bfloat16)
    halved = jnp.concatenate([halved, jnp.zeros((PADDED - ncomp, nblk * bs), jnp.bfloat16)], axis=0)
    source_rows = jnp.transpose(halved.reshape(PADDED, nblk, bs), (1, 2, 0))
    flat_slots = pair_slots.reshape(-1)

    vmem = 48 * 1024 * 1024
    scratch = [pltpu.VMEM((nslot, 1, bs), jnp.float32), pltpu.VMEM((chunks, bs, CHUNK * bs), jnp.float32)]
    sweep = pl.pallas_call(
        functools.partial(sweep_kernel, most=most, log_mass=log_mass, ncomp=ncomp),
        out_shape=(jax.ShapeDtypeStruct((nslot, 1, bs), jnp.float32),) * 2,
        in_specs=_specs("ssvvv"),
        out_specs=tuple(_specs("vv")),
        scratch_shapes=scratch,
        compiler_params=pltpu.CompilerParams(vmem_limit_bytes=vmem),
    )
    final = pl.pallas_call(
        functools.partial(final_kernel, most=most, log_mass=log_mass, ncomp=ncomp),
        out_shape=(
            jax.ShapeDtypeStruct((nblk, 1, bs), jnp.float32),
            jax.ShapeDtypeStruct((ncomp, nblk * bs), jnp.float32),
        ),
        in_specs=_specs("ssvvvvv"),
        out_specs=tuple(_specs("vv")),
        scratch_shapes=scratch,
        compiler_params=pltpu.CompilerParams(vmem_limit_bytes=vmem),
    )

    owned = asked_local[:, None] == jnp.arange(nblk, dtype=jnp.int32)[None, :]
    for sweep_index in range(SWEEPS):
        part_max, part_sum = sweep(flat_slots, pair_counts, source_rows, slot_coords, slot_potential)
        parts = jnp.stack([part_max.reshape(nslot, bs), part_sum.reshape(nslot, bs)], axis=1)
        came = lax.all_to_all(
            parts.reshape(peers, cap, 2, bs), "blocks", split_axis=0, concat_axis=0, tiled=True
        ).reshape(nslot, 2, bs)
        came_max = came[:, 0]
        came_sum = came[:, 1]
        merged = jnp.max(jnp.where(owned[:, :, None], came_max[:, None, :], floor_value), axis=0)
        scaled = came_sum[:, None, :] * jnp.exp(came_max[:, None, :] - merged[None, :, :])
        summed = jnp.sum(jnp.where(owned[:, :, None], scaled, 0.0), axis=0)
        reached = merged > 0.5 * floor_value
        potential_here = jnp.where(
            reached, log_mass - (merged + jnp.log(jnp.where(reached, summed, 1.0))), potential_here
        )
        send_potential = potential_here[asked_local].reshape(peers, cap, bs)
        slot_potential = lax.all_to_all(
            send_potential, "blocks", split_axis=0, concat_axis=0, tiled=True
        ).reshape(nslot, 1, bs)

    source_side, drift = final(
        flat_slots, pair_counts, source_rows, source_coords, slot_coords, slot_rows, slot_potential
    )
    return (source_side.reshape(-1), potential_here.reshape(-1), drift)


def solution(mesh):
    return jax.shard_map(
        local,
        mesh=mesh,
        in_specs=(
            P(None, ("groups", "blocks")),
            P(None, ("groups", "blocks")),
            P(("groups", "blocks")),
            P(("groups", "blocks"), None, None),
            P(("groups", "blocks"), None),
            P(("groups", "blocks")),
        ),
        out_specs=(P(("groups", "blocks")), P(("groups", "blocks")), P(None, ("groups", "blocks"))),
        check_vma=False,
    )
```

time: 213 us -> 135 us (0.63)
  the two profiles are of different devices: /device:TPU:11 before, /device:TPU:0 now
where the time goes in v2:
time: 135 us; the launch traced here: 133 us
  Pallas kernels  48.7 us (36%)
  waiting for transfers between devices  35.8 us (27%)
  starting transfers between devices  25.7 us (19%)
  blocking collectives  9.07 us (7%)
  local copies, waits for them, and re-layouts  8.85 us (7%)
  other arithmetic  4.13 us (3%)
    pallas_call x2, Pallas kernels, local(): sweep(flat_slots, pair_counts, source_rows, slot_coords, slot_potential)  31.1 us
    pallas_call x1, Pallas kernels, local(): final(flat_slots, pair_counts, source_rows, source_coords, slot_coords, s...  17.6 us
    all_to_all x1, waiting for transfers between devices, local(): lax.all_to_all(send, 'blocks', split_axis=0, concat_axis=0, tiled=True)  12.8 us
    all_to_all x2, waiting for transfers between devices, local(): lax.all_to_all(parts.reshape(peers, cap, 2, bs), 'blocks', split_axis=0,...  12.4 us
    all_to_all x2, starting transfers between devices, local(): lax.all_to_all(parts.reshape(peers, cap, 2, bs), 'blocks', split_axis=0,...  11.1 us
    all_to_all x1, blocking collectives, local(): lax.all_to_all(send_potential, 'blocks', split_axis=0, concat_axis=0, til...  9.07 us
    all_to_all x1, starting transfers between devices, local(): lax.all_to_all(wanted, 'blocks', split_axis=0, concat_axis=0, tiled=True)  7.41 us
    all_to_all x1, waiting for transfers between devices, local(): lax.all_to_all(send_potential, 'blocks', split_axis=0, concat_axis=0, til...  5.86 us
  transfers between devices with their start and end apart: 5, of which 5 were waited for; matrix products, arithmetic and copies ran while one was open for 2% of the time, Pallas kernels for 0%

profile of v2, /device:TPU:0, one launch (start us, length us, event | category | flops | bytes accessed | tf_op | source)
XLA Modules:
  0.0 133.1 jit_solution(5467124839403285355)
XLA Ops:
  0.6 0.0 copy-start.4
  0.6 0.7 copy-done.4
  1.3 0.7 copy.42
  2.0 7.4 %all-to-all-start = ((s32[16,1,2]{2,1,0:T(1,128)}), s32[16,1,2]{2,1,0:T(1,128)S(1)}, u32[]{:S(2)}, u32[]{:S(2)}) async-start(s32[16,1,2]{2,1,0:T(1,128)} %copy.42), calls=%async_computation | async-start | bytes 16384 | tf_op jit(solution)/shard_map/all_to_all | solution.py:155
  9.4 0.9 transpose.29
  10.3 0.0 copy-start.2
  10.4 0.6 copy-done.2
  11.0 4.7 %all-to-all-done = s32[16,1,2]{2,1,0:T(1,128)S(1)} async-done(((s32[16,1,2]{2,1,0:T(1,128)}), s32[16,1,2]{2,1,0:T(1,128)S(1)}, u32[]{:S(2)}, u32[]{:S(2)}) %all-to-all-start) | async-done | bytes 160 | tf_op jit(solution)/shard_map/all_to_all | solution.py:155
  15.8 0.5 broadcast.142
  16.3 0.7 reduce.5
  17.0 0.1 all_to_all.27
  17.1 0.6 gather_fusion
  17.7 1.2 copy.43
  18.9 0.0 copy-start
  18.9 3.7 %all-to-all-start.1 = ((f32[16,2,31,128]{3,1,2,0:T(2,128)}), f32[16,2,31,128]{3,1,2,0:T(2,128)S(1)}, u32[]{:S(2)}, u32[]{:S(2)}) async-start(f32[16,2,31,128]{3,1,2,0:T(2,128)} %copy.43), calls=%async_computation.1 | async-start | bytes 1015808 | tf_op jit(solution)/shard_map/all_to_all | solution.py:164
  22.6 0.0 copy-start.3
  22.6 0.1 pad.8.clone
  22.7 0.1 pad.7.clone
  22.7 0.5 copy-done.3
  23.3 0.1 reshape.151.slots_ref
  23.3 0.0 copy-done
  23.4 0.2 copy.54
  23.5 0.1 concatenate.12.clone
  23.6 0.1 all_to_all.29
  23.7 12.8 %all-to-all-done.1 = f32[16,2,31,128]{3,1,2,0:T(2,128)S(1)} async-done(((f32[16,2,31,128]{3,1,2,0:T(2,128)}), f32[16,2,31,128]{3,1,2,0:T(2,128)S(1)}, u32[]{:S(2)}, u32[]{:S(2)}) %all-to-all-start.1) | async-done | bytes 507936 | tf_op jit(solution)/shard_map/all_to_all | solution.py:164
  36.5 0.1 copy.44
  36.7 0.1 maximum_maximum_fusion.y_ref
  36.8 0.0 copy-start.1
  36.8 0.6 copy-done.1
  37.5 15.5 %shard_map.85 = (f32[32,1,128]{2,1,0:T(1,128)S(1)}, f32[32,1,128]{2,1,0:T(1,128)S(1)}) custom-call(s32[256]{0:T(256)S(1)} %reshape.151.slots_ref, s32[8]{0:T(128)S(1)} %copy-done.1, bf16[8,128,32]{2,1,0:T(8,128)(2,1)S(1)} %bitcast.68, bf16[32,32,128]{2,1,0:T(8,128)(2,1)S(1)} %maximum_maximum_fusion.y_ref, f32[32,1,128]{2,1,0:T(1,128)S(1)} %slice.32.g_ref), custom_call_target="tpu_custom_call" | custom-call | tf_op jit(solution)/shard_map/pallas_call | solution.py:207
  53.0 0.6 pad_maximum_fusion.1
  53.7 6.1 %all-to-all-start.2 = ((f32[16,2,2,128]{3,2,1,0:T(2,128)}), f32[16,2,2,128]{3,2,1,0:T(2,128)S(1)}, u32[]{:S(2)}, u32[]{:S(2)}) async-start(f32[16,2,2,128]{3,2,1,0:T(2,128)} %bitcast.10), calls=%async_computation.2 | async-start | bytes 65536 | tf_op jit(solution)/shard_map/all_to_all | solution.py:209
  59.8 0.1 iota_compare_fusion
  59.8 6.6 %all-to-all-done.2 = f32[16,2,2,128]{3,2,1,0:T(2,128)S(1)} async-done(((f32[16,2,2,128]{3,2,1,0:T(2,128)}), f32[16,2,2,128]{3,2,1,0:T(2,128)S(1)}, u32[]{:S(2)}, u32[]{:S(2)}) %all-to-all-start.2) | async-done | bytes 32800 | tf_op jit(solution)/shard_map/all_to_all | solution.py:209
  66.4 0.1 select_reduce_fusion.3
  66.5 0.1 select_reduce_fusion.2
  66.7 0.6 gather_fusion.1
  67.2 9.1 %all_to_all.40 = f32[16,2,128]{2,1,0:T(2,128)S(1)} all-to-all(f32[16,2,128]{2,1,0:T(2,128)S(1)} %bitcast.83), channel_id=1, replica_groups=mesh['groups'=2,'blocks'=16] {'blocks'}, dimensions={0} | all-to-all | bytes 32768 | tf_op jit(solution)/shard_map/all_to_all | solution.py:222
  76.3 15.5 %shard_map.86 = (f32[32,1,128]{2,1,0:T(1,128)S(1)}, f32[32,1,128]{2,1,0:T(1,128)S(1)}) custom-call(s32[256]{0:T(256)S(1)} %reshape.151.slots_ref, s32[8]{0:T(128)S(1)} %copy-done.1, bf16[8,128,32]{2,1,0:T(8,128)(2,1)S(1)} %bitcast.69, bf16[32,32,128]{2,1,0:T(8,128)(2,1)S(1)} %maximum_maximum_fusion.y_ref, f32[32,1,128]{2,1,0:T(1,128)S(1)} %bitcast.72), custom_call_target="tpu_custom_call" | custom-call | tf_op jit(solution)/shard_map/pallas_call | solution.py:207
  91.8 0.6 pad_maximum_fusion.2
  92.5 5.0 %all-to-all-start.4 = ((f32[16,2,2,128]{3,2,1,0:T(2,128)}), f32[16,2,2,128]{3,2,1,0:T(2,128)S(1)}, u32[]{:S(2)}, u32[]{:S(2)}) async-start(f32[16,2,2,128]{3,2,1,0:T(2,128)} %bitcast.17), calls=%async_computation.4 | async-start | bytes 65536 | tf_op jit(solution)/shard_map/all_to_all | solution.py:209
  97.5 0.5 copy.45
  98.0 0.3 concatenate.15.yT_ref
  98.3 5.9 %all-to-all-done.4 = f32[16,2,2,128]{3,2,1,0:T(2,128)S(1)} async-done(((f32[16,2,2,128]{3,2,1,0:T(2,128)}), f32[16,2,2,128]{3,2,1,0:T(2,128)S(1)}, u32[]{:S(2)}, u32[]{:S(2)}) %all-to-all-start.4) | async-done | bytes 32800 | tf_op jit(solution)/shard_map/all_to_all | solution.py:209
  104.1 0.1 select_reduce_fusion.1
  104.2 0.1 select_reduce_fusion
  104.4 1.2 gather_fusion.2
  105.5 3.5 %all-to-all-start.5 = ((f32[16,2,128]{2,1,0:T(2,128)}), f32[16,2,128]{2,1,0:T(2,128)S(1)}, u32[]{:S(2)}, u32[]{:S(2)}) async-start(f32[16,2,128]{2,1,0:T(2,128)} %bitcast.21), calls=%async_computation.5 | async-start | bytes 32768 | tf_op jit(solution)/shard_map/all_to_all | solution.py:222
  109.0 0.6 fusion.4
  109.6 5.9 %all-to-all-done.5 = f32[16,2,128]{2,1,0:T(2,128)S(1)} async-done(((f32[16,2,128]{2,1,0:T(2,128)}), f32[16,2,128]{2,1,0:T(2,128)S(1)}, u32[]{:S(2)}, u32[]{:S(2)}) %all-to-all-start.5) | async-done | bytes 16416 | tf_op jit(solution)/shard_map/all_to_all | solution.py:222
  115.5 17.6 %shard_map.87 = (f32[8,1,128]{2,1,0:T(1,128)}, f32[30,1024]{1,0:T(8,128)}) custom-call(s32[256]{0:T(256)S(1)} %reshape.151.slots_ref, s32[8]{0:T(128)S(1)} %copy-done.1, bf16[8,128,32]{2,1,0:T(8,128)(2,1)S(1)} %bitcast.70, bf16[30,1024]{1,0:T(8,128)(2,1)S(1)} %copy-done, bf16[32,32,128]{2,1,0:T(8,128)(2,1)S(1)} %maximum_maximum_fusion.y_ref, ...), custom_call_target="tpu_custom_call" | custom-call | tf_op jit(solution)/shard_map/pallas_call | solution.py:226
  (14 shorter events, 0.3 us)
Async XLA Ops:
  0.6 0.7 copy-start.4
  2.0 13.8 %all-to-all-start = ((s32[16,1,2]{2,1,0:T(1,128)}), s32[16,1,2]{2,1,0:T(1,128)S(1)}, u32[]{:S(2)}, u32[]{:S(2)}) async-start(s32[16,1,2]{2,1,0:T(1,128)} %copy.42), calls=%async_computation | async-start | bytes 16384 | tf_op jit(solution)/shard_map/all_to_all | solution.py:155
  10.3 0.7 copy-start.2
  18.9 4.5 %copy-start = (bf16[30,1024]{1,0:T(8,128)(2,1)S(1)}, bf16[30,1024]{1,0:T(8,128)(2,1)}, u32[]{:S(2)}) copy-start(bf16[30,1024]{1,0:T(8,128)(2,1)} %x_ref.1) | copy-start | bytes 184324
  18.9 17.7 %all-to-all-start.1 = ((f32[16,2,31,128]{3,1,2,0:T(2,128)}), f32[16,2,31,128]{3,1,2,0:T(2,128)S(1)}, u32[]{:S(2)}, u32[]{:S(2)}) async-start(f32[16,2,31,128]{3,1,2,0:T(2,128)} %copy.43), calls=%async_computation.1 | async-start | bytes 1015808 | tf_op jit(solution)/shard_map/all_to_all | solution.py:164
  22.6 0.7 copy-start.3
  36.8 0.7 copy-start.1
  53.7 12.7 %all-to-all-start.2 = ((f32[16,2,2,128]{3,2,1,0:T(2,128)}), f32[16,2,2,128]{3,2,1,0:T(2,128)S(1)}, u32[]{:S(2)}, u32[]{:S(2)}) async-start(f32[16,2,2,128]{3,2,1,0:T(2,128)} %bitcast.10), calls=%async_computation.2 | async-start | bytes 65536 | tf_op jit(solution)/shard_map/all_to_all | solution.py:209
  92.5 11.6 %all-to-all-start.4 = ((f32[16,2,2,128]{3,2,1,0:T(2,128)}), f32[16,2,2,128]{3,2,1,0:T(2,128)S(1)}, u32[]{:S(2)}, u32[]{:S(2)}) async-start(f32[16,2,2,128]{3,2,1,0:T(2,128)} %bitcast.17), calls=%async_computation.4 | async-start | bytes 65536 | tf_op jit(solution)/shard_map/all_to_all | solution.py:209
  105.5 10.0 %all-to-all-start.5 = ((f32[16,2,128]{2,1,0:T(2,128)}), f32[16,2,128]{2,1,0:T(2,128)S(1)}, u32[]{:S(2)}, u32[]{:S(2)}) async-start(f32[16,2,128]{2,1,0:T(2,128)} %bitcast.21), calls=%async_computation.5 | async-start | bytes 32768 | tf_op jit(solution)/shard_map/all_to_all | solution.py:222

commit v3 on v2

--- a/solution.py
+++ b/solution.py
@@ -12,7 +12,7 @@
 
 floor_value = -1e30
 PADDED = 32
-CHUNK = 4
+CHUNK = 8
 
 
 def _slot_offsets(y_ref, g_ref, h_ref, ncomp):
@@ -46,8 +46,8 @@
         sls = _chunk_slots(slots_ref, s, q, most)
         rhs = jnp.concatenate([y_ref[sl] for sl in sls], axis=1)
         hrow = jnp.concatenate([h_ref[sl] for sl in sls], axis=1)
-        prod = jnp.dot(xs, rhs, preferred_element_type=jnp.float32)
-        sc = jnp.where(lane_tile + q * CHUNK < cnt, prod + hrow, floor_value)
+        hrow = jnp.where(lane_tile + q * CHUNK < cnt, hrow, floor_value)
+        sc = jnp.dot(xs, rhs, preferred_element_type=jnp.float32) + hrow
         s_ref[q] = sc
         return jnp.maximum(m, _lane_fold(sc, bs, jnp.maximum))
 
@@ -80,13 +80,13 @@
             cm = jnp.max(v, axis=0, keepdims=True)
             ce = jnp.sum(jnp.exp(v - cm), axis=0, keepdims=True)
             for t, sl in enumerate(sls):
-                @pl.when(q * CHUNK + t < cnt)
-                def _():
-                    tm = cm[:, t * bs : (t + 1) * bs] - g_ref[sl]
-                    om = amax_ref[sl]
-                    nm = jnp.maximum(om, tm)
-                    asum_ref[sl] = asum_ref[sl] * jnp.exp(om - nm) + ce[:, t * bs : (t + 1) * bs] * jnp.exp(tm - nm)
-                    amax_ref[sl] = nm
+                valid = q * CHUNK + t < cnt
+                tm = jnp.where(valid, cm[:, t * bs : (t + 1) * bs] - g_ref[sl], floor_value)
+                te = jnp.where(valid, ce[:, t * bs : (t + 1) * bs], 0.0)
+                om = amax_ref[sl]
+                nm = jnp.maximum(om, tm)
+                asum_ref[sl] = asum_ref[sl] * jnp.exp(om - nm) + te * jnp.exp(tm - nm)
+                amax_ref[sl] = nm
             return c
 
         lax.fori_loop(0, nq, column, 0)

time: 135 us -> 124 us (0.919)
  the two profiles are of different devices: /device:TPU:0 before, /device:TPU:10 now
where the time goes in v3:
time: 124 us; the launch traced here: 123 us
  Pallas kernels  42.8 us (35%)
  waiting for transfers between devices  29.1 us (23%)
  starting transfers between devices  27.9 us (22%)
  blocking collectives  9.18 us (7%)
  local copies, waits for them, and re-layouts  8.85 us (7%)
  other arithmetic  4.12 us (3%)
    pallas_call x2, Pallas kernels, local(): sweep(flat_slots, pair_counts, source_rows, slot_coords, slot_potential)  27.9 us
    pallas_call x1, Pallas kernels, local(): final(flat_slots, pair_counts, source_rows, source_coords, slot_coords, s...  14.9 us
    all_to_all x1, waiting for transfers between devices, local(): lax.all_to_all(send, 'blocks', split_axis=0, concat_axis=0, tiled=True)  12.1 us
    all_to_all x2, starting transfers between devices, local(): lax.all_to_all(parts.reshape(peers, cap, 2, bs), 'blocks', split_axis=0,...  11.6 us
    all_to_all x2, waiting for transfers between devices, local(): lax.all_to_all(parts.reshape(peers, cap, 2, bs), 'blocks', split_axis=0,...  9.25 us
    all_to_all x1, blocking collectives, local(): lax.all_to_all(send_potential, 'blocks', split_axis=0, concat_axis=0, til...  9.18 us
    all_to_all x1, starting transfers between devices, local(): lax.all_to_all(wanted, 'blocks', split_axis=0, concat_axis=0, tiled=True)  6.3 us
    all_to_all x1, starting transfers between devices, local(): lax.all_to_all(send, 'blocks', split_axis=0, concat_axis=0, tiled=True)  5.03 us
  transfers between devices with their start and end apart: 5, of which 5 were waited for; matrix products, arithmetic and copies ran while one was open for 2% of the time, Pallas kernels for 0%

profile of v3, /device:TPU:10, one launch (start us, length us, event | category | flops | bytes accessed | tf_op | source)
XLA Modules:
  0.0 122.8 jit_solution(9348762739263414372)
XLA Ops:
  0.6 0.0 copy-start.4
  0.6 0.7 copy-done.4
  1.3 0.7 copy.42
  2.0 6.3 %all-to-all-start = ((s32[16,1,2]{2,1,0:T(1,128)}), s32[16,1,2]{2,1,0:T(1,128)S(1)}, u32[]{:S(2)}, u32[]{:S(2)}) async-start(s32[16,1,2]{2,1,0:T(1,128)} %copy.42), calls=%async_computation | async-start | bytes 16384 | tf_op jit(solution)/shard_map/all_to_all | solution.py:155
  8.3 0.8 transpose.29
  9.2 0.0 copy-start.2
  9.2 0.6 copy-done.2
  9.9 3.3 %all-to-all-done = s32[16,1,2]{2,1,0:T(1,128)S(1)} async-done(((s32[16,1,2]{2,1,0:T(1,128)}), s32[16,1,2]{2,1,0:T(1,128)S(1)}, u32[]{:S(2)}, u32[]{:S(2)}) %all-to-all-start) | async-done | bytes 160 | tf_op jit(solution)/shard_map/all_to_all | solution.py:155
  13.2 0.5 broadcast.142
  13.7 0.7 reduce.5
  14.4 0.1 all_to_all.27
  14.5 0.6 gather_fusion
  15.1 1.2 copy.43
  16.3 0.0 copy-start
  16.3 5.0 %all-to-all-start.1 = ((f32[16,2,31,128]{3,1,2,0:T(2,128)}), f32[16,2,31,128]{3,1,2,0:T(2,128)S(1)}, u32[]{:S(2)}, u32[]{:S(2)}) async-start(f32[16,2,31,128]{3,1,2,0:T(2,128)} %copy.43), calls=%async_computation.1 | async-start | bytes 1015808 | tf_op jit(solution)/shard_map/all_to_all | solution.py:164
  21.3 0.0 copy-start.3
  21.3 0.1 pad.8.clone
  21.4 0.1 pad.7.clone
  21.5 0.5 copy-done.3
  22.0 0.1 reshape.151.slots_ref
  22.1 0.0 copy-done
  22.1 0.2 copy.54
  22.3 0.1 concatenate.12.clone
  22.4 0.1 all_to_all.29
  22.5 12.1 %all-to-all-done.1 = f32[16,2,31,128]{3,1,2,0:T(2,128)S(1)} async-done(((f32[16,2,31,128]{3,1,2,0:T(2,128)}), f32[16,2,31,128]{3,1,2,0:T(2,128)S(1)}, u32[]{:S(2)}, u32[]{:S(2)}) %all-to-all-start.1) | async-done | bytes 507936 | tf_op jit(solution)/shard_map/all_to_all | solution.py:164
  34.5 0.1 copy.44
  34.7 0.1 maximum_maximum_fusion.y_ref
  34.8 0.0 copy-start.1
  34.8 0.6 copy-done.1
  35.5 14.0 %shard_map.85 = (f32[32,1,128]{2,1,0:T(1,128)S(1)}, f32[32,1,128]{2,1,0:T(1,128)S(1)}) custom-call(s32[256]{0:T(256)S(1)} %reshape.151.slots_ref, s32[8]{0:T(128)S(1)} %copy-done.1, bf16[8,128,32]{2,1,0:T(8,128)(2,1)S(1)} %bitcast.68, bf16[32,32,128]{2,1,0:T(8,128)(2,1)S(1)} %maximum_maximum_fusion.y_ref, f32[32,1,128]{2,1,0:T(1,128)S(1)} %slice.32.g_ref), custom_call_target="tpu_custom_call" | custom-call | tf_op jit(solution)/shard_map/pallas_call | solution.py:207
  49.5 0.6 pad_maximum_fusion.1
  50.1 5.9 %all-to-all-start.2 = ((f32[16,2,2,128]{3,2,1,0:T(2,128)}), f32[16,2,2,128]{3,2,1,0:T(2,128)S(1)}, u32[]{:S(2)}, u32[]{:S(2)}) async-start(f32[16,2,2,128]{3,2,1,0:T(2,128)} %bitcast.10), calls=%async_computation.2 | async-start | bytes 65536 | tf_op jit(solution)/shard_map/all_to_all | solution.py:209
  56.0 0.1 iota_compare_fusion
  56.1 5.0 %all-to-all-done.2 = f32[16,2,2,128]{3,2,1,0:T(2,128)S(1)} async-done(((f32[16,2,2,128]{3,2,1,0:T(2,128)}), f32[16,2,2,128]{3,2,1,0:T(2,128)S(1)}, u32[]{:S(2)}, u32[]{:S(2)}) %all-to-all-start.2) | async-done | bytes 32800 | tf_op jit(solution)/shard_map/all_to_all | solution.py:209
  61.1 0.1 select_reduce_fusion.3
  61.2 0.1 select_reduce_fusion.2
  61.3 0.6 gather_fusion.1
  61.9 9.2 %all_to_all.40 = f32[16,2,128]{2,1,0:T(2,128)S(1)} all-to-all(f32[16,2,128]{2,1,0:T(2,128)S(1)} %bitcast.83), channel_id=1, replica_groups=mesh['groups'=2,'blocks'=16] {'blocks'}, dimensions={0} | all-to-all | bytes 32768 | tf_op jit(solution)/shard_map/all_to_all | solution.py:222
  71.1 14.0 %shard_map.86 = (f32[32,1,128]{2,1,0:T(1,128)S(1)}, f32[32,1,128]{2,1,0:T(1,128)S(1)}) custom-call(s32[256]{0:T(256)S(1)} %reshape.151.slots_ref, s32[8]{0:T(128)S(1)} %copy-done.1, bf16[8,128,32]{2,1,0:T(8,128)(2,1)S(1)} %bitcast.69, bf16[32,32,128]{2,1,0:T(8,128)(2,1)S(1)} %maximum_maximum_fusion.y_ref, f32[32,1,128]{2,1,0:T(1,128)S(1)} %bitcast.72), custom_call_target="tpu_custom_call" | custom-call | tf_op jit(solution)/shard_map/pallas_call | solution.py:207
  85.1 0.6 pad_maximum_fusion.2
  85.7 5.7 %all-to-all-start.4 = ((f32[16,2,2,128]{3,2,1,0:T(2,128)}), f32[16,2,2,128]{3,2,1,0:T(2,128)S(1)}, u32[]{:S(2)}, u32[]{:S(2)}) async-start(f32[16,2,2,128]{3,2,1,0:T(2,128)} %bitcast.17), calls=%async_computation.4 | async-start | bytes 65536 | tf_op jit(solution)/shard_map/all_to_all | solution.py:209
  91.4 0.5 copy.45
  91.9 0.3 concatenate.15.yT_ref
  92.2 4.3 %all-to-all-done.4 = f32[16,2,2,128]{3,2,1,0:T(2,128)S(1)} async-done(((f32[16,2,2,128]{3,2,1,0:T(2,128)}), f32[16,2,2,128]{3,2,1,0:T(2,128)S(1)}, u32[]{:S(2)}, u32[]{:S(2)}) %all-to-all-start.4) | async-done | bytes 32800 | tf_op jit(solution)/shard_map/all_to_all | solution.py:209
  96.5 0.1 select_reduce_fusion.1
  96.6 0.1 select_reduce_fusion
  96.7 1.2 gather_fusion.2
  97.9 5.0 %all-to-all-start.5 = ((f32[16,2,128]{2,1,0:T(2,128)}), f32[16,2,128]{2,1,0:T(2,128)S(1)}, u32[]{:S(2)}, u32[]{:S(2)}) async-start(f32[16,2,128]{2,1,0:T(2,128)} %bitcast.21), calls=%async_computation.5 | async-start | bytes 32768 | tf_op jit(solution)/shard_map/all_to_all | solution.py:222
  102.9 0.6 fusion.4
  103.5 4.5 %all-to-all-done.5 = f32[16,2,128]{2,1,0:T(2,128)S(1)} async-done(((f32[16,2,128]{2,1,0:T(2,128)}), f32[16,2,128]{2,1,0:T(2,128)S(1)}, u32[]{:S(2)}, u32[]{:S(2)}) %all-to-all-start.5) | async-done | bytes 16416 | tf_op jit(solution)/shard_map/all_to_all | solution.py:222
  108.0 14.9 %shard_map.87 = (f32[8,1,128]{2,1,0:T(1,128)}, f32[30,1024]{1,0:T(8,128)}) custom-call(s32[256]{0:T(256)S(1)} %reshape.151.slots_ref, s32[8]{0:T(128)S(1)} %copy-done.1, bf16[8,128,32]{2,1,0:T(8,128)(2,1)S(1)} %bitcast.70, bf16[30,1024]{1,0:T(8,128)(2,1)S(1)} %copy-done, bf16[32,32,128]{2,1,0:T(8,128)(2,1)S(1)} %maximum_maximum_fusion.y_ref, ...), custom_call_target="tpu_custom_call" | custom-call | tf_op jit(solution)/shard_map/pallas_call | solution.py:226
  (14 shorter events, 0.3 us)
Async XLA Ops:
  0.6 0.7 copy-start.4
  2.0 11.2 %all-to-all-start = ((s32[16,1,2]{2,1,0:T(1,128)}), s32[16,1,2]{2,1,0:T(1,128)S(1)}, u32[]{:S(2)}, u32[]{:S(2)}) async-start(s32[16,1,2]{2,1,0:T(1,128)} %copy.42), calls=%async_computation | async-start | bytes 16384 | tf_op jit(solution)/shard_map/all_to_all | solution.py:155
  9.2 0.7 copy-start.2
  16.3 5.8 %copy-start = (bf16[30,1024]{1,0:T(8,128)(2,1)S(1)}, bf16[30,1024]{1,0:T(8,128)(2,1)}, u32[]{:S(2)}) copy-start(bf16[30,1024]{1,0:T(8,128)(2,1)} %x_ref.1) | copy-start | bytes 184324
  16.3 18.2 %all-to-all-start.1 = ((f32[16,2,31,128]{3,1,2,0:T(2,128)}), f32[16,2,31,128]{3,1,2,0:T(2,128)S(1)}, u32[]{:S(2)}, u32[]{:S(2)}) async-start(f32[16,2,31,128]{3,1,2,0:T(2,128)} %copy.43), calls=%async_computation.1 | async-start | bytes 1015808 | tf_op jit(solution)/shard_map/all_to_all | solution.py:164
  21.3 0.7 copy-start.3
  34.8 0.7 copy-start.1
  50.1 10.9 %all-to-all-start.2 = ((f32[16,2,2,128]{3,2,1,0:T(2,128)}), f32[16,2,2,128]{3,2,1,0:T(2,128)S(1)}, u32[]{:S(2)}, u32[]{:S(2)}) async-start(f32[16,2,2,128]{3,2,1,0:T(2,128)} %bitcast.10), calls=%async_computation.2 | async-start | bytes 65536 | tf_op jit(solution)/shard_map/all_to_all | solution.py:209
  85.7 10.7 %all-to-all-start.4 = ((f32[16,2,2,128]{3,2,1,0:T(2,128)}), f32[16,2,2,128]{3,2,1,0:T(2,128)S(1)}, u32[]{:S(2)}, u32[]{:S(2)}) async-start(f32[16,2,2,128]{3,2,1,0:T(2,128)} %bitcast.17), calls=%async_computation.4 | async-start | bytes 65536 | tf_op jit(solution)/shard_map/all_to_all | solution.py:209
  97.9 10.1 %all-to-all-start.5 = ((f32[16,2,128]{2,1,0:T(2,128)}), f32[16,2,128]{2,1,0:T(2,128)S(1)}, u32[]{:S(2)}, u32[]{:S(2)}) async-start(f32[16,2,128]{2,1,0:T(2,128)} %bitcast.21), calls=%async_computation.5 | async-start | bytes 32768 | tf_op jit(solution)/shard_map/all_to_all | solution.py:222

commit v4 on v3

--- a/solution.py
+++ b/solution.py
@@ -32,11 +32,8 @@
     return [slots_ref[s * most + jnp.minimum(q * CHUNK + c, most - 1)] for c in range(CHUNK)]
 
 
-def _lane_fold(v, bs, op):
-    out = v[:, 0:bs]
-    for c in range(1, CHUNK):
-        out = op(out, v[:, c * bs : (c + 1) * bs])
-    return out
+def _rows_of(values):
+    return jnp.concatenate(values, axis=0)
 
 
 def _row_scores(s, cnt, slots_ref, xs, y_ref, h_ref, s_ref, most, bs):
@@ -48,8 +45,11 @@
         hrow = jnp.concatenate([h_ref[sl] for sl in sls], axis=1)
         hrow = jnp.where(lane_tile + q * CHUNK < cnt, hrow, floor_value)
         sc = jnp.dot(xs, rhs, preferred_element_type=jnp.float32) + hrow
-        s_ref[q] = sc
-        return jnp.maximum(m, _lane_fold(sc, bs, jnp.maximum))
+        for t in range(CHUNK):
+            tile = sc[:, t * bs : (t + 1) * bs]
+            s_ref[q, :, t * bs : (t + 1) * bs] = tile
+            m = jnp.maximum(m, tile)
+        return m
 
     nq = (cnt + CHUNK - 1) // CHUNK
     m = lax.fori_loop(0, nq, first, jnp.full((bs, bs), floor_value, jnp.float32))
@@ -61,32 +61,40 @@
     _slot_offsets(y_ref, g_ref, h_ref, ncomp)
     amax_ref[...] = jnp.full(amax_ref.shape, floor_value, jnp.float32)
     asum_ref[...] = jnp.zeros(asum_ref.shape, jnp.float32)
+    tile_row = lax.broadcasted_iota(jnp.int32, (CHUNK, bs), 0)
 
     def block(s, carry):
         cnt = counts_ref[s]
         nq, mrow = _row_scores(s, cnt, slots_ref, xT_ref[s], y_ref, h_ref, s_ref, most, bs)
-        mb = jnp.concatenate([jnp.broadcast_to(mrow, (bs, bs))] * CHUNK, axis=1)
+        mb = jnp.broadcast_to(mrow, (bs, bs))
 
         def second(q, acc):
-            return acc + _lane_fold(jnp.exp(s_ref[q] - mb), bs, jnp.add)
+            for t in range(CHUNK):
+                acc = acc + jnp.exp(s_ref[q, :, t * bs : (t + 1) * bs] - mb)
+            return acc
 
         acc = lax.fori_loop(0, nq, second, jnp.zeros((bs, bs), jnp.float32))
         tot = jnp.sum(acc, axis=1, keepdims=True)
-        kb = jnp.concatenate([jnp.broadcast_to(log_mass - (mrow + jnp.log(tot)), (bs, bs))] * CHUNK, axis=1)
+        kb = jnp.broadcast_to(log_mass - (mrow + jnp.log(tot)), (bs, bs))
 
         def column(q, c):
             sls = _chunk_slots(slots_ref, s, q, most)
-            v = s_ref[q] + kb
-            cm = jnp.max(v, axis=0, keepdims=True)
-            ce = jnp.sum(jnp.exp(v - cm), axis=0, keepdims=True)
+            cms, ces = [], []
+            for t in range(CHUNK):
+                v = s_ref[q, :, t * bs : (t + 1) * bs] + kb
+                cm = jnp.max(v, axis=0, keepdims=True)
+                cms.append(cm)
+                ces.append(jnp.sum(jnp.exp(v - cm), axis=0, keepdims=True))
+            valid = tile_row + q * CHUNK < cnt
+            tm = jnp.where(valid, _rows_of(cms) - _rows_of([g_ref[sl] for sl in sls]), floor_value)
+            te = jnp.where(valid, _rows_of(ces), 0.0)
+            om = _rows_of([amax_ref[sl] for sl in sls])
+            os = _rows_of([asum_ref[sl] for sl in sls])
+            nm = jnp.maximum(om, tm)
+            ns = os * jnp.exp(om - nm) + te * jnp.exp(tm - nm)
             for t, sl in enumerate(sls):
-                valid = q * CHUNK + t < cnt
-                tm = jnp.where(valid, cm[:, t * bs : (t + 1) * bs] - g_ref[sl], floor_value)
-                te = jnp.where(valid, ce[:, t * bs : (t + 1) * bs], 0.0)
-                om = amax_ref[sl]
-                nm = jnp.maximum(om, tm)
-                asum_ref[sl] = asum_ref[sl] * jnp.exp(om - nm) + te * jnp.exp(tm - nm)
-                amax_ref[sl] = nm
+                amax_ref[sl] = nm[t : t + 1]
+                asum_ref[sl] = ns[t : t + 1]
             return c
 
         lax.fori_loop(0, nq, column, 0)
@@ -104,16 +112,16 @@
         cnt = counts_ref[s]
         xs = xT_ref[s]
         nq, mrow = _row_scores(s, cnt, slots_ref, xs, y_ref, h_ref, s_ref, most, bs)
-        mb = jnp.concatenate([jnp.broadcast_to(mrow, (bs, bs))] * CHUNK, axis=1)
+        mb = jnp.broadcast_to(mrow, (bs, bs))
 
         def second(q, c):
             acc, num = c
             sls = _chunk_slots(slots_ref, s, q, most)
-            e = jnp.exp(s_ref[q] - mb)
-            w = e.astype(jnp.bfloat16)
-            rhs = jnp.concatenate([yT_ref[sl] for sl in sls], axis=0)
-            num = num + jnp.dot(w, rhs, preferred_element_type=jnp.float32)
-            return acc + _lane_fold(e, bs, jnp.add), num
+            for t, sl in enumerate(sls):
+                e = jnp.exp(s_ref[q, :, t * bs : (t + 1) * bs] - mb)
+                acc = acc + e
+                num = num + jnp.dot(e.astype(jnp.bfloat16), yT_ref[sl], preferred_element_type=jnp.float32)
+            return acc, num
 
         acc, num = lax.fori_loop(
             0,
@@ -149,7 +157,8 @@
     nslot = peers * cap
     most = pair_slots.shape[1]
     log_mass = -math.log(peers * nblk * bs)
-    chunks = (most + CHUNK - 1) // CHUNK
+    chunks = most // CHUNK
+    assert most % CHUNK == 0
 
     wanted = fetch_blocks[0]
     asked = lax.all_to_all(wanted, "blocks", split_axis=0, concat_axis=0, tiled=True)

time: 124 us -> 122 us (0.984)
  the two profiles are of different devices: /device:TPU:10 before, /device:TPU:0 now
where the time goes in v4:
time: 122 us; the launch traced here: 124 us
  Pallas kernels  42.8 us (35%)
  waiting for transfers between devices  35.8 us (29%)
  starting transfers between devices  22.2 us (18%)
  blocking collectives  9.07 us (7%)
  local copies, waits for them, and re-layouts  8.85 us (7%)
  other arithmetic  4.13 us (3%)
    pallas_call x2, Pallas kernels, local(): sweep(flat_slots, pair_counts, source_rows, slot_coords, slot_potential)  27.6 us
    pallas_call x1, Pallas kernels, local(): final(flat_slots, pair_counts, source_rows, source_coords, slot_coords, s...  15.2 us
    all_to_all x1, waiting for transfers between devices, local(): lax.all_to_all(send, 'blocks', split_axis=0, concat_axis=0, tiled=True)  12.8 us
    all_to_all x2, waiting for transfers between devices, local(): lax.all_to_all(parts.reshape(peers, cap, 2, bs), 'blocks', split_axis=0,...  12.4 us
    all_to_all x1, blocking collectives, local(): lax.all_to_all(send_potential, 'blocks', split_axis=0, concat_axis=0, til...  9.07 us
    all_to_all x2, starting transfers between devices, local(): lax.all_to_all(parts.reshape(peers, cap, 2, bs), 'blocks', split_axis=0,...  7.61 us
    all_to_all x1, starting transfers between devices, local(): lax.all_to_all(wanted, 'blocks', split_axis=0, concat_axis=0, tiled=True)  7.41 us
    all_to_all x1, waiting for transfers between devices, local(): lax.all_to_all(send_potential, 'blocks', split_axis=0, concat_axis=0, til...  5.86 us
  transfers between devices with their start and end apart: 5, of which 5 were waited for; matrix products, arithmetic and copies ran while one was open for 2% of the time, Pallas kernels for 0%

profile of v4, /device:TPU:0, one launch (start us, length us, event | category | flops | bytes accessed | tf_op | source)
XLA Modules:
  0.0 123.7 jit_solution(2091927011775669801)
XLA Ops:
  0.6 0.0 copy-start.4
  0.6 0.7 copy-done.4
  1.3 0.7 copy.42
  2.0 7.4 %all-to-all-start = ((s32[16,1,2]{2,1,0:T(1,128)}), s32[16,1,2]{2,1,0:T(1,128)S(1)}, u32[]{:S(2)}, u32[]{:S(2)}) async-start(s32[16,1,2]{2,1,0:T(1,128)} %copy.42), calls=%async_computation | async-start | bytes 16384 | tf_op jit(solution)/shard_map/all_to_all | solution.py:164
  9.4 0.9 transpose.29
  10.3 0.0 copy-start.2
  10.4 0.6 copy-done.2
  11.0 4.7 %all-to-all-done = s32[16,1,2]{2,1,0:T(1,128)S(1)} async-done(((s32[16,1,2]{2,1,0:T(1,128)}), s32[16,1,2]{2,1,0:T(1,128)S(1)}, u32[]{:S(2)}, u32[]{:S(2)}) %all-to-all-start) | async-done | bytes 160 | tf_op jit(solution)/shard_map/all_to_all | solution.py:164
  15.8 0.5 broadcast.142
  16.3 0.7 reduce.5
  17.0 0.1 all_to_all.27
  17.1 0.6 gather_fusion
  17.7 1.2 copy.43
  18.9 0.0 copy-start
  18.9 3.7 %all-to-all-start.1 = ((f32[16,2,31,128]{3,1,2,0:T(2,128)}), f32[16,2,31,128]{3,1,2,0:T(2,128)S(1)}, u32[]{:S(2)}, u32[]{:S(2)}) async-start(f32[16,2,31,128]{3,1,2,0:T(2,128)} %copy.43), calls=%async_computation.1 | async-start | bytes 1015808 | tf_op jit(solution)/shard_map/all_to_all | solution.py:173
  22.6 0.0 copy-start.3
  22.6 0.1 pad.8.clone
  22.7 0.1 pad.7.clone
  22.7 0.5 copy-done.3
  23.3 0.1 reshape.151.slots_ref
  23.3 0.0 copy-done
  23.4 0.2 copy.54
  23.5 0.1 concatenate.12.clone
  23.6 0.1 all_to_all.29
  23.7 12.8 %all-to-all-done.1 = f32[16,2,31,128]{3,1,2,0:T(2,128)S(1)} async-done(((f32[16,2,31,128]{3,1,2,0:T(2,128)}), f32[16,2,31,128]{3,1,2,0:T(2,128)S(1)}, u32[]{:S(2)}, u32[]{:S(2)}) %all-to-all-start.1) | async-done | bytes 507936 | tf_op jit(solution)/shard_map/all_to_all | solution.py:173
  36.5 0.1 copy.44
  36.7 0.1 maximum_maximum_fusion.y_ref
  36.8 0.0 copy-start.1
  36.8 0.6 copy-done.1
  37.5 13.8 %shard_map.85 = (f32[32,1,128]{2,1,0:T(1,128)S(1)}, f32[32,1,128]{2,1,0:T(1,128)S(1)}) custom-call(s32[256]{0:T(256)S(1)} %reshape.151.slots_ref, s32[8]{0:T(128)S(1)} %copy-done.1, bf16[8,128,32]{2,1,0:T(8,128)(2,1)S(1)} %bitcast.68, bf16[32,32,128]{2,1,0:T(8,128)(2,1)S(1)} %maximum_maximum_fusion.y_ref, f32[32,1,128]{2,1,0:T(1,128)S(1)} %slice.32.g_ref), custom_call_target="tpu_custom_call" | custom-call | tf_op jit(solution)/shard_map/pallas_call | solution.py:216
  51.3 0.6 pad_maximum_fusion.1
  51.9 4.1 %all-to-all-start.2 = ((f32[16,2,2,128]{3,2,1,0:T(2,128)}), f32[16,2,2,128]{3,2,1,0:T(2,128)S(1)}, u32[]{:S(2)}, u32[]{:S(2)}) async-start(f32[16,2,2,128]{3,2,1,0:T(2,128)} %bitcast.10), calls=%async_computation.2 | async-start | bytes 65536 | tf_op jit(solution)/shard_map/all_to_all | solution.py:218
  56.1 0.1 iota_compare_fusion
  56.1 6.6 %all-to-all-done.2 = f32[16,2,2,128]{3,2,1,0:T(2,128)S(1)} async-done(((f32[16,2,2,128]{3,2,1,0:T(2,128)}), f32[16,2,2,128]{3,2,1,0:T(2,128)S(1)}, u32[]{:S(2)}, u32[]{:S(2)}) %all-to-all-start.2) | async-done | bytes 32800 | tf_op jit(solution)/shard_map/all_to_all | solution.py:218
  62.7 0.1 select_reduce_fusion.3
  62.8 0.1 select_reduce_fusion.2
  63.0 0.6 gather_fusion.1
  63.5 9.1 %all_to_all.40 = f32[16,2,128]{2,1,0:T(2,128)S(1)} all-to-all(f32[16,2,128]{2,1,0:T(2,128)S(1)} %bitcast.83), channel_id=1, replica_groups=mesh['groups'=2,'blocks'=16] {'blocks'}, dimensions={0} | all-to-all | bytes 32768 | tf_op jit(solution)/shard_map/all_to_all | solution.py:231
  72.6 13.8 %shard_map.86 = (f32[32,1,128]{2,1,0:T(1,128)S(1)}, f32[32,1,128]{2,1,0:T(1,128)S(1)}) custom-call(s32[256]{0:T(256)S(1)} %reshape.151.slots_ref, s32[8]{0:T(128)S(1)} %copy-done.1, bf16[8,128,32]{2,1,0:T(8,128)(2,1)S(1)} %bitcast.69, bf16[32,32,128]{2,1,0:T(8,128)(2,1)S(1)} %maximum_maximum_fusion.y_ref, f32[32,1,128]{2,1,0:T(1,128)S(1)} %bitcast.72), custom_call_target="tpu_custom_call" | custom-call | tf_op jit(solution)/shard_map/pallas_call | solution.py:216
  86.4 0.6 pad_maximum_fusion.2
  87.1 3.5 %all-to-all-start.4 = ((f32[16,2,2,128]{3,2,1,0:T(2,128)}), f32[16,2,2,128]{3,2,1,0:T(2,128)S(1)}, u32[]{:S(2)}, u32[]{:S(2)}) async-start(f32[16,2,2,128]{3,2,1,0:T(2,128)} %bitcast.17), calls=%async_computation.4 | async-start | bytes 65536 | tf_op jit(solution)/shard_map/all_to_all | solution.py:218
  90.6 0.5 copy.45
  91.1 0.3 concatenate.15.yT_ref
  91.4 5.8 %all-to-all-done.4 = f32[16,2,2,128]{3,2,1,0:T(2,128)S(1)} async-done(((f32[16,2,2,128]{3,2,1,0:T(2,128)}), f32[16,2,2,128]{3,2,1,0:T(2,128)S(1)}, u32[]{:S(2)}, u32[]{:S(2)}) %all-to-all-start.4) | async-done | bytes 32800 | tf_op jit(solution)/shard_map/all_to_all | solution.py:218
  97.2 0.1 select_reduce_fusion.1
  97.3 0.1 select_reduce_fusion
  97.4 1.2 gather_fusion.2
  98.6 3.5 %all-to-all-start.5 = ((f32[16,2,128]{2,1,0:T(2,128)}), f32[16,2,128]{2,1,0:T(2,128)S(1)}, u32[]{:S(2)}, u32[]{:S(2)}) async-start(f32[16,2,128]{2,1,0:T(2,128)} %bitcast.21), calls=%async_computation.5 | async-start | bytes 32768 | tf_op jit(solution)/shard_map/all_to_all | solution.py:231
  102.1 0.6 fusion.4
  102.7 5.9 %all-to-all-done.5 = f32[16,2,128]{2,1,0:T(2,128)S(1)} async-done(((f32[16,2,128]{2,1,0:T(2,128)}), f32[16,2,128]{2,1,0:T(2,128)S(1)}, u32[]{:S(2)}, u32[]{:S(2)}) %all-to-all-start.5) | async-done | bytes 16416 | tf_op jit(solution)/shard_map/all_to_all | solution.py:231
  108.6 15.2 %shard_map.87 = (f32[8,1,128]{2,1,0:T(1,128)}, f32[30,1024]{1,0:T(8,128)}) custom-call(s32[256]{0:T(256)S(1)} %reshape.151.slots_ref, s32[8]{0:T(128)S(1)} %copy-done.1, bf16[8,128,32]{2,1,0:T(8,128)(2,1)S(1)} %bitcast.70, bf16[30,1024]{1,0:T(8,128)(2,1)S(1)} %copy-done, bf16[32,32,128]{2,1,0:T(8,128)(2,1)S(1)} %maximum_maximum_fusion.y_ref, ...), custom_call_target="tpu_custom_call" | custom-call | tf_op jit(solution)/shard_map/pallas_call | solution.py:235
  (14 shorter events, 0.3 us)
Async XLA Ops:
  0.6 0.7 copy-start.4
  2.0 13.8 %all-to-all-start = ((s32[16,1,2]{2,1,0:T(1,128)}), s32[16,1,2]{2,1,0:T(1,128)S(1)}, u32[]{:S(2)}, u32[]{:S(2)}) async-start(s32[16,1,2]{2,1,0:T(1,128)} %copy.42), calls=%async_computation | async-start | bytes 16384 | tf_op jit(solution)/shard_map/all_to_all | solution.py:164
  10.3 0.7 copy-start.2
  18.9 4.5 %copy-start = (bf16[30,1024]{1,0:T(8,128)(2,1)S(1)}, bf16[30,1024]{1,0:T(8,128)(2,1)}, u32[]{:S(2)}) copy-start(bf16[30,1024]{1,0:T(8,128)(2,1)} %x_ref.1) | copy-start | bytes 184324
  18.9 17.7 %all-to-all-start.1 = ((f32[16,2,31,128]{3,1,2,0:T(2,128)}), f32[16,2,31,128]{3,1,2,0:T(2,128)S(1)}, u32[]{:S(2)}, u32[]{:S(2)}) async-start(f32[16,2,31,128]{3,1,2,0:T(2,128)} %copy.43), calls=%async_computation.1 | async-start | bytes 1015808 | tf_op jit(solution)/shard_map/all_to_all | solution.py:173
  22.6 0.7 copy-start.3
  36.8 0.7 copy-start.1
  51.9 10.8 %all-to-all-start.2 = ((f32[16,2,2,128]{3,2,1,0:T(2,128)}), f32[16,2,2,128]{3,2,1,0:T(2,128)S(1)}, u32[]{:S(2)}, u32[]{:S(2)}) async-start(f32[16,2,2,128]{3,2,1,0:T(2,128)} %bitcast.10), calls=%async_computation.2 | async-start | bytes 65536 | tf_op jit(solution)/shard_map/all_to_all | solution.py:218
  87.1 10.1 %all-to-all-start.4 = ((f32[16,2,2,128]{3,2,1,0:T(2,128)}), f32[16,2,2,128]{3,2,1,0:T(2,128)S(1)}, u32[]{:S(2)}, u32[]{:S(2)}) async-start(f32[16,2,2,128]{3,2,1,0:T(2,128)} %bitcast.17), calls=%async_computation.4 | async-start | bytes 65536 | tf_op jit(solution)/shard_map/all_to_all | solution.py:218
  98.6 10.0 %all-to-all-start.5 = ((f32[16,2,128]{2,1,0:T(2,128)}), f32[16,2,128]{2,1,0:T(2,128)S(1)}, u32[]{:S(2)}, u32[]{:S(2)}) async-start(f32[16,2,128]{2,1,0:T(2,128)} %bitcast.21), calls=%async_computation.5 | async-start | bytes 32768 | tf_op jit(solution)/shard_map/all_to_all | solution.py:231

commit v5 on v4

--- a/solution.py
+++ b/solution.py
@@ -56,7 +56,7 @@
     return nq, jnp.max(m, axis=1, keepdims=True)
 
 
-def sweep_kernel(slots_ref, counts_ref, xT_ref, y_ref, g_ref, amax_ref, asum_ref, h_ref, s_ref, *, most, log_mass, ncomp):
+def sweep_kernel(slots_ref, counts_ref, xT_ref, y_ref, g_ref, lse_ref, amax_ref, asum_ref, h_ref, s_ref, *, most, log_mass, ncomp):
     nblk, bs = xT_ref.shape[0], xT_ref.shape[1]
     _slot_offsets(y_ref, g_ref, h_ref, ncomp)
     amax_ref[...] = jnp.full(amax_ref.shape, floor_value, jnp.float32)
@@ -102,6 +102,13 @@
 
     lax.fori_loop(0, nblk, block, 0)
 
+    def finish(t, c):
+        am = amax_ref[t]
+        lse_ref[t] = jnp.where(am > 0.5 * floor_value, am + jnp.log(asum_ref[t]), floor_value)
+        return c
+
+    lax.fori_loop(0, lse_ref.shape[0], finish, 0)
+
 
 def final_kernel(slots_ref, counts_ref, xT_ref, x_ref, y_ref, yT_ref, g_ref, f_ref, drift_ref, h_ref, s_ref, *, most, log_mass, ncomp):
     nblk, bs = xT_ref.shape[0], xT_ref.shape[1]
@@ -161,7 +168,11 @@
     assert most % CHUNK == 0
 
     wanted = fetch_blocks[0]
-    asked = lax.all_to_all(wanted, "blocks", split_axis=0, concat_axis=0, tiled=True)
+    me = lax.axis_index("blocks")
+    fetch_all = lax.all_to_all(
+        jnp.broadcast_to(wanted[None], (peers, peers, cap)), "blocks", split_axis=0, concat_axis=0, tiled=True
+    )
+    asked = lax.dynamic_index_in_dim(fetch_all, me, axis=1, keepdims=False)
     asked_local = (asked % nblk).reshape(-1)
 
     potential_here = target_potential.reshape(nblk, bs)
@@ -193,10 +204,10 @@
     scratch = [pltpu.VMEM((nslot, 1, bs), jnp.float32), pltpu.VMEM((chunks, bs, CHUNK * bs), jnp.float32)]
     sweep = pl.pallas_call(
         functools.partial(sweep_kernel, most=most, log_mass=log_mass, ncomp=ncomp),
-        out_shape=(jax.ShapeDtypeStruct((nslot, 1, bs), jnp.float32),) * 2,
+        out_shape=jax.ShapeDtypeStruct((nslot, 1, bs), jnp.float32),
         in_specs=_specs("ssvvv"),
-        out_specs=tuple(_specs("vv")),
-        scratch_shapes=scratch,
+        out_specs=_specs("v")[0],
+        scratch_shapes=[pltpu.VMEM((nslot, 1, bs), jnp.float32)] * 2 + scratch,
         compiler_params=pltpu.CompilerParams(vmem_limit_bytes=vmem),
     )
     final = pl.pallas_call(
@@ -211,26 +222,38 @@
         compiler_params=pltpu.CompilerParams(vmem_limit_bytes=vmem),
     )
 
-    owned = asked_local[:, None] == jnp.arange(nblk, dtype=jnp.int32)[None, :]
+    def combine(values, match, previous, axes):
+        merged = jnp.max(jnp.where(match, values, floor_value), axis=axes)
+        summed = jnp.sum(jnp.where(match, jnp.exp(values - jnp.expand_dims(merged, axes)), 0.0), axis=axes)
+        reached = merged > 0.5 * floor_value
+        return jnp.where(reached, log_mass - (merged + jnp.log(jnp.where(reached, summed, 1.0))), previous)
+
+    owned = (asked_local.reshape(peers, cap)[None] == jnp.arange(nblk, dtype=jnp.int32)[:, None, None])[..., None]
+    gather_all = peers * nslot * bs * 4 <= (1 << 20)
+    if gather_all:
+        fetched = jnp.transpose(fetch_all, (1, 0, 2))[:, None, :, :] == wanted[:, :, None, None]
+        fetched = fetched[..., None]
     for sweep_index in range(SWEEPS):
-        part_max, part_sum = sweep(flat_slots, pair_counts, source_rows, slot_coords, slot_potential)
-        parts = jnp.stack([part_max.reshape(nslot, bs), part_sum.reshape(nslot, bs)], axis=1)
-        came = lax.all_to_all(
-            parts.reshape(peers, cap, 2, bs), "blocks", split_axis=0, concat_axis=0, tiled=True
-        ).reshape(nslot, 2, bs)
-        came_max = came[:, 0]
-        came_sum = came[:, 1]
-        merged = jnp.max(jnp.where(owned[:, :, None], came_max[:, None, :], floor_value), axis=0)
-        scaled = came_sum[:, None, :] * jnp.exp(came_max[:, None, :] - merged[None, :, :])
-        summed = jnp.sum(jnp.where(owned[:, :, None], scaled, 0.0), axis=0)
-        reached = merged > 0.5 * floor_value
-        potential_here = jnp.where(
-            reached, log_mass - (merged + jnp.log(jnp.where(reached, summed, 1.0))), potential_here
-        )
-        send_potential = potential_here[asked_local].reshape(peers, cap, bs)
-        slot_potential = lax.all_to_all(
-            send_potential, "blocks", split_axis=0, concat_axis=0, tiled=True
-        ).reshape(nslot, 1, bs)
+        lse = sweep(flat_slots, pair_counts, source_rows, slot_coords, slot_potential).reshape(nslot, bs)
+        if gather_all:
+            came = lax.all_to_all(
+                jnp.broadcast_to(lse[None], (peers, nslot, bs)), "blocks", split_axis=0, concat_axis=0, tiled=True
+            ).reshape(peers, peers, cap, bs)
+            mine = lax.dynamic_index_in_dim(came, me, axis=1, keepdims=False)
+            potential_here = combine(mine[None], owned, potential_here, (1, 2))
+            by_owner = jnp.transpose(came, (1, 0, 2, 3))[:, None]
+            slot_potential = combine(
+                by_owner, fetched, slot_potential.reshape(peers, cap, bs), (2, 3)
+            ).reshape(nslot, 1, bs)
+        else:
+            came = lax.all_to_all(
+                lse.reshape(peers, cap, bs), "blocks", split_axis=0, concat_axis=0, tiled=True
+            )
+            potential_here = combine(came[None], owned, potential_here, (1, 2))
+            send_potential = potential_here[asked_local].reshape(peers, cap, bs)
+            slot_potential = lax.all_to_all(
+                send_potential, "blocks", split_axis=0, concat_axis=0, tiled=True
+            ).reshape(nslot, 1, bs)
 
     source_side, drift = final(
         flat_slots, pair_counts, source_rows, source_coords, slot_coords, slot_rows, slot_potential

time: 122 us -> 109 us (0.89); the launches traced: 124 us -> 108 us
  blocking collectives: 9.07 us -> 0 us
  Pallas kernels: 42.8 us -> 37.9 us
  starting transfers between devices: 22.2 us -> 20.9 us
    all_to_all x1 -> x0, blocking collectives: 9.07 us -> none  [local(): lax.all_to_all(send_potential, 'blocks', split_axis=0, concat_axis=0, til...]
    pallas_call x2, Pallas kernels: 27.6 us -> 24.5 us  [local(): sweep(flat_slots, pair_counts, source_rows, slot_coords, slot_potential)]
    broadcast_in_dim x0 -> x5, local copies, waits for them, and re-layouts: none -> 2.16 us  [the longest x2 1.45 us: local(): jnp.broadcast_to(lse[None], (peers, nslot, bs))]
    pallas_call x1, Pallas kernels: 15.2 us -> 13.4 us  [local(): final(flat_slots, pair_counts, source_rows, source_coords, slot_coords, s...]
    gather x2 -> x0, local copies, waits for them, and re-layouts: 1.74 us -> none  [local(): send_potential = potential_here[asked_local].reshape(peers, cap, bs)]
    all_to_all x4 -> x3, starting transfers between devices: 18.5 us -> 17.2 us  [the longest x2 9.74 us: local(): lax.all_to_all(jnp.broadcast_to(lse[None], (peers, nslot, bs)), 'blocks',...]
    another operation x2 -> x0, other arithmetic: 1.3 us -> none  [local(): jnp.stack([part_max.reshape(nslot, bs), part_sum.reshape(nslot, bs)], axi...]
    all_to_all x4 -> x3, waiting for transfers between devices: 23 us -> 23.6 us  [the longest x2 18.7 us: local(): lax.all_to_all(jnp.broadcast_to(lse[None], (peers, nslot, bs)), 'blocks',...]
  transfers between devices with their start and end apart: 5 -> 4, of which waited for: 5 -> 4; matrix products, arithmetic and copies ran while one was open for 2% -> 2% of each run, Pallas kernels for 0% -> 0%
where the time goes in v5:
time: 109 us; the launch traced here: 108 us
  Pallas kernels  37.9 us (35%)
  waiting for transfers between devices  36.5 us (33%)
  starting transfers between devices  20.9 us (19%)
  local copies, waits for them, and re-layouts  8.85 us (8%)
  other arithmetic  3.3 us (3%)
    pallas_call x2, Pallas kernels, local(): sweep(flat_slots, pair_counts, source_rows, slot_coords, slot_potential)  24.5 us
    all_to_all x2, waiting for transfers between devices, local(): lax.all_to_all(jnp.broadcast_to(lse[None], (peers, nslot, bs)), 'blocks',...  18.7 us
    pallas_call x1, Pallas kernels, local(): final(flat_slots, pair_counts, source_rows, source_coords, slot_coords, s...  13.4 us
    all_to_all x1, waiting for transfers between devices, local(): lax.all_to_all(send, 'blocks', split_axis=0, concat_axis=0, tiled=True)  12.9 us
    all_to_all x2, starting transfers between devices, local(): lax.all_to_all(jnp.broadcast_to(lse[None], (peers, nslot, bs)), 'blocks',...  9.74 us
    all_to_all x1, starting transfers between devices, local(): lax.all_to_all(jnp.broadcast_to(wanted[None], (peers, peers, cap)), 'bloc...  7.41 us
    all_to_all x1, waiting for transfers between devices, local(): lax.all_to_all(jnp.broadcast_to(wanted[None], (peers, peers, cap)), 'bloc...  4.88 us
    all_to_all x1, starting transfers between devices, local(): lax.all_to_all(send, 'blocks', split_axis=0, concat_axis=0, tiled=True)  3.7 us
  transfers between devices with their start and end apart: 4, of which 4 were waited for; matrix products, arithmetic and copies ran while one was open for 2% of the time, Pallas kernels for 0%

profile of v5, /device:TPU:0, one launch (start us, length us, event | category | flops | bytes accessed | tf_op | source)
XLA Modules:
  0.0 108.4 jit_solution(13609060205749364806)
XLA Ops:
  0.6 0.0 copy-start.3
  0.6 0.7 copy-done.3
  1.3 0.6 broadcast_in_dim.143
  1.9 7.4 %all-to-all-start = ((s32[16,16,2]{1,2,0:T(2,128)}), s32[16,16,2]{1,2,0:T(2,128)S(1)}, u32[]{:S(2)}, u32[]{:S(2)}) async-start(s32[16,16,2]{1,2,0:T(2,128)} %broadcast_in_dim.143), calls=%async_computation | async-start | bytes 32768 | tf_op jit(solution)/shard_map/all_to_all | solution.py:172
  9.3 0.9 transpose.49
  10.2 0.0 copy-start.2
  10.3 0.6 copy-done.2
  11.0 4.9 %all-to-all-done = s32[16,16,2]{1,2,0:T(2,128)S(1)} async-done(((s32[16,16,2]{1,2,0:T(2,128)}), s32[16,16,2]{1,2,0:T(2,128)S(1)}, u32[]{:S(2)}, u32[]{:S(2)}) %all-to-all-start) | async-done | bytes 2080 | tf_op jit(solution)/shard_map/all_to_all | solution.py:172
  15.8 0.4 fusion.15
  16.3 0.1 squeeze.9
  16.4 0.6 gather_fusion
  17.0 1.2 %copy.71 = f32[16,2,31,128]{3,1,2,0:T(2,128)} copy(f32[16,2,31,128]{3,2,1,0:T(8,128)S(1)} %bitcast.76) | data formatting | bytes 1015808 | tf_op jit(solution)/shard_map/reshape | solution.py:183
  18.2 0.0 copy-start
  18.2 3.7 %all-to-all-start.1 = ((f32[16,2,31,128]{3,1,2,0:T(2,128)}), f32[16,2,31,128]{3,1,2,0:T(2,128)S(1)}, u32[]{:S(2)}, u32[]{:S(2)}) async-start(f32[16,2,31,128]{3,1,2,0:T(2,128)} %copy.71), calls=%async_computation.1 | async-start | bytes 1015808 | tf_op jit(solution)/shard_map/all_to_all | solution.py:184
  21.9 0.0 copy-start.4
  21.9 0.1 pad.4.clone
  22.0 0.1 pad.3.clone
  22.0 0.5 copy-done.4
  22.6 0.1 reshape.220.slots_ref
  22.6 0.0 copy-done
  22.7 0.2 copy.79
  22.9 0.1 concatenate.12.clone
  22.9 12.9 %all-to-all-done.1 = f32[16,2,31,128]{3,1,2,0:T(2,128)S(1)} async-done(((f32[16,2,31,128]{3,1,2,0:T(2,128)}), f32[16,2,31,128]{3,1,2,0:T(2,128)S(1)}, u32[]{:S(2)}, u32[]{:S(2)}) %all-to-all-start.1) | async-done | bytes 507936 | tf_op jit(solution)/shard_map/all_to_all | solution.py:184
  35.9 0.1 copy.72
  36.0 0.1 maximum_maximum_fusion.y_ref
  36.1 0.0 copy-start.1
  36.1 0.6 copy-done.1
  36.8 12.3 %shard_map.85 = f32[32,1,128]{2,1,0:T(1,128)S(1)} custom-call(s32[256]{0:T(256)S(1)} %reshape.220.slots_ref, s32[8]{0:T(128)S(1)} %copy-done.1, bf16[8,128,32]{2,1,0:T(8,128)(2,1)S(1)} %bitcast.65, bf16[32,32,128]{2,1,0:T(8,128)(2,1)S(1)} %maximum_maximum_fusion.y_ref, f32[32,1,128]{2,1,0:T(1,128)S(1)} %slice.12.g_ref), custom_call_target="tpu_custom_call" | custom-call | tf_op jit(solution)/shard_map/pallas_call | solution.py:237
  49.1 0.7 broadcast_in_dim.148
  49.8 5.4 %all-to-all-start.2 = ((f32[16,32,128]{2,1,0:T(8,128)}), f32[16,32,128]{2,1,0:T(8,128)S(1)}, u32[]{:S(2)}, u32[]{:S(2)}) async-start(f32[16,32,128]{2,1,0:T(8,128)} %broadcast_in_dim.148), calls=%async_computation.2 | async-start | bytes 524288 | tf_op jit(solution)/shard_map/all_to_all | solution.py:239
  55.2 0.1 copy.74
  55.3 0.1 copy.73
  55.4 0.1 copy.78
  55.5 0.1 broadcast_compare_fusion
  55.6 9.6 %all-to-all-done.2 = f32[16,32,128]{2,1,0:T(8,128)S(1)} async-done(((f32[16,32,128]{2,1,0:T(8,128)}), f32[16,32,128]{2,1,0:T(8,128)S(1)}, u32[]{:S(2)}, u32[]{:S(2)}) %all-to-all-start.2) | async-done | bytes 262176 | tf_op jit(solution)/shard_map/all_to_all | solution.py:239
  65.2 0.2 copy.75
  65.4 0.2 select_reduce_fusion.3
  65.6 0.2 select_reduce_fusion.2
  65.9 0.1 compare_select_fusion.2.g_ref
  65.9 12.3 %shard_map.86 = f32[32,1,128]{2,1,0:T(1,128)S(1)} custom-call(s32[256]{0:T(256)S(1)} %reshape.220.slots_ref, s32[8]{0:T(128)S(1)} %copy-done.1, bf16[8,128,32]{2,1,0:T(8,128)(2,1)S(1)} %bitcast.66, bf16[32,32,128]{2,1,0:T(8,128)(2,1)S(1)} %maximum_maximum_fusion.y_ref, f32[32,1,128]{2,1,0:T(1,128)S(1)} %compare_select_fusion.2.g_ref), custom_call_target="tpu_custom_call" | custom-call | tf_op jit(solution)/shard_map/pallas_call | solution.py:237
  78.2 0.7 broadcast_in_dim.154
  78.9 4.3 %all-to-all-start.3 = ((f32[16,32,128]{2,1,0:T(8,128)}), f32[16,32,128]{2,1,0:T(8,128)S(1)}, u32[]{:S(2)}, u32[]{:S(2)}) async-start(f32[16,32,128]{2,1,0:T(8,128)} %broadcast_in_dim.154), calls=%async_computation.3 | async-start | bytes 524288 | tf_op jit(solution)/shard_map/all_to_all | solution.py:239
  83.3 0.1 fusion.16
  83.4 0.5 copy.80
  83.9 0.3 concatenate.15.clone.yT_ref
  84.2 9.1 %all-to-all-done.3 = f32[16,32,128]{2,1,0:T(8,128)S(1)} async-done(((f32[16,32,128]{2,1,0:T(8,128)}), f32[16,32,128]{2,1,0:T(8,128)S(1)}, u32[]{:S(2)}, u32[]{:S(2)}) %all-to-all-start.3) | async-done | bytes 262176 | tf_op jit(solution)/shard_map/all_to_all | solution.py:239
  93.3 0.2 copy.76
  93.5 0.1 select_reduce_fusion.7
  93.6 0.1 select_reduce_fusion.6
  93.7 0.1 select_reduce_fusion.4
  93.8 0.2 select_reduce_fusion.1
  94.1 0.2 select_reduce_fusion
  94.3 0.6 fusion.8
  94.9 0.1 compare_select_fusion.g_ref
  95.0 13.4 %shard_map.87 = (f32[8,1,128]{2,1,0:T(1,128)}, f32[30,1024]{1,0:T(8,128)}) custom-call(s32[256]{0:T(256)S(1)} %reshape.220.slots_ref, s32[8]{0:T(128)S(1)} %copy-done.1, bf16[8,128,32]{2,1,0:T(8,128)(2,1)S(1)} %bitcast.67, bf16[30,1024]{1,0:T(8,128)(2,1)S(1)} %copy-done, bf16[32,32,128]{2,1,0:T(8,128)(2,1)S(1)} %maximum_maximum_fusion.y_ref, ...), custom_call_target="tpu_custom_call" | custom-call | tf_op jit(solution)/shard_map/pallas_call | solution.py:258
  (12 shorter events, 0.2 us)
Async XLA Ops:
  0.6 0.7 copy-start.3
  1.9 13.9 %all-to-all-start = ((s32[16,16,2]{1,2,0:T(2,128)}), s32[16,16,2]{1,2,0:T(2,128)S(1)}, u32[]{:S(2)}, u32[]{:S(2)}) async-start(s32[16,16,2]{1,2,0:T(2,128)} %broadcast_in_dim.143), calls=%async_computation | async-start | bytes 32768 | tf_op jit(solution)/shard_map/all_to_all | solution.py:172
  10.2 0.7 copy-start.2
  18.2 4.5 %copy-start = (bf16[30,1024]{1,0:T(8,128)(2,1)S(1)}, bf16[30,1024]{1,0:T(8,128)(2,1)}, u32[]{:S(2)}) copy-start(bf16[30,1024]{1,0:T(8,128)(2,1)} %x_ref.1) | copy-start | bytes 184324
  18.2 17.7 %all-to-all-start.1 = ((f32[16,2,31,128]{3,1,2,0:T(2,128)}), f32[16,2,31,128]{3,1,2,0:T(2,128)S(1)}, u32[]{:S(2)}, u32[]{:S(2)}) async-start(f32[16,2,31,128]{3,1,2,0:T(2,128)} %copy.71), calls=%async_computation.1 | async-start | bytes 1015808 | tf_op jit(solution)/shard_map/all_to_all | solution.py:184
  21.9 0.7 copy-start.4
  36.1 0.7 copy-start.1
  49.8 15.4 %all-to-all-start.2 = ((f32[16,32,128]{2,1,0:T(8,128)}), f32[16,32,128]{2,1,0:T(8,128)S(1)}, u32[]{:S(2)}, u32[]{:S(2)}) async-start(f32[16,32,128]{2,1,0:T(8,128)} %broadcast_in_dim.148), calls=%async_computation.2 | async-start | bytes 524288 | tf_op jit(solution)/shard_map/all_to_all | solution.py:239
  78.9 14.3 %all-to-all-start.3 = ((f32[16,32,128]{2,1,0:T(8,128)}), f32[16,32,128]{2,1,0:T(8,128)S(1)}, u32[]{:S(2)}, u32[]{:S(2)}) async-start(f32[16,32,128]{2,1,0:T(8,128)} %broadcast_in_dim.154), calls=%async_computation.3 | async-start | bytes 524288 | tf_op jit(solution)/shard_map/all_to_all | solution.py:239
